TPU v7x, 512 devices: a whole 4x4x16 slice. The times are simulated.
512 devices in a mesh: adapter: 64 (over y, z), mp: 8 (over x, core).
Axes of the slice: x: 4, y: 4, z: 16, core: 2. Of those that a mesh axis runs over, the one named last changes fastest.
Arguments:
- tokens: bfloat16 [24576, 8192], P('adapter', 'mp'), may hold values from -6 to 6
- cotangent: bfloat16 [24576, 1024], P('adapter', 'mp'), may hold values from -6 to 6
- value_weight: bfloat16 [8192, 1024], P('mp', 'adapter'), may hold values from -0.0625 to 0.0625
- down_store: bfloat16 [128, 8, 1024, 64], P(None, 'mp', 'adapter'), may hold values from -0.0625 to 0.0625
- down_first: float32 [128, 8, 1024, 64], P(None, 'mp', 'adapter'), may hold values from -4 to 4
- down_second: float32 [128, 8, 1024, 64], P(None, 'mp', 'adapter'), may hold values from 0.01 to 1
- up_store: bfloat16 [128, 64, 1024], P(None, 'adapter', 'mp'), may hold values from -0.75 to 0.75
- up_first: float32 [128, 64, 1024], P(None, 'adapter', 'mp'), may hold values from -4 to 4
- up_second: float32 [128, 64, 1024], P(None, 'adapter', 'mp'), may hold values from 0.01 to 1
- tile_adapter: int32 [192], replicated, may hold values from 0 to 127
- tile_length: int32 [192], replicated, may hold values from 1 to 128, as said below
- adapter_slot: int32 [128], replicated, may hold values from 0 to 127, each once
Outputs:
- projected: bfloat16 [24576, 1024], P('adapter', 'mp')
- token_gradient: bfloat16 [24576, 8192], P('adapter', 'mp')
- new_down: float32 [128, 8, 1024, 64], P(None, 'mp', 'adapter')
- new_down_first: float32 [128, 8, 1024, 64], P(None, 'mp', 'adapter')
- new_down_second: float32 [128, 8, 1024, 64], P(None, 'mp', 'adapter')
- new_up: float32 [128, 64, 1024], P(None, 'adapter', 'mp')
- new_up_first: float32 [128, 64, 1024], P(None, 'adapter', 'mp')
- new_up_second: float32 [128, 64, 1024], P(None, 'adapter', 'mp')
Inputs may be any that keep to these rules, and one draw needn't show every extreme that they name: `tile_length`: some tile is full in every draw. `adapter_slot`: each slot holds exactly one adapter.
All inputs are finite; a program needn't handle non-finite values.
Results may differ from a plain program's by a relative error of at most 0.0046.
Values may be sent and summed in bfloat16 or wider, within the bound.
No kernel may reach another device: no remote copies, remote signals or barrier semaphores. Data moves between devices by JAX's collectives and lax.ppermute only.
A program may use at most 64 MiB of HBM per device.

v0:
```python
import jax
import jax.numpy as jnp
from jax import lax
from jax.sharding import PartitionSpec as P

TILE = 128
STEP = 100


adapter_scale = 2.0
learn_rate = 0.001
beta_one = 0.9
beta_two = 0.999
adam_eps = 1e-08


def adam_step(store, first, second, gradient):
    new_first = beta_one * first + (1.0 - beta_one) * gradient
    new_second = beta_two * second + (1.0 - beta_two) * gradient * gradient
    corr_one = 1.0 - beta_one**STEP
    corr_two = 1.0 - beta_two**STEP
    moved = store.astype(jnp.float32) - learn_rate * (new_first / corr_one) / (
        jnp.sqrt(new_second / corr_two) + adam_eps
    )
    return (moved, new_first, new_second)


def shards(
    tokens,
    cotangent,
    value_weight,
    down_store,
    down_first,
    down_second,
    up_store,
    up_first,
    up_second,
    tile_adapter,
    tile_length,
    adapter_slot,
):
    tile_total = tile_adapter.shape[0]
    tok_count, feat_part = tokens.shape
    head_cols = cotangent.shape[1]
    tiles_here = tok_count // TILE
    adapter_count = adapter_slot.shape[0]
    my_index = lax.axis_index("adapter")
    adapter_ids = jnp.arange(adapter_count, dtype=jnp.int32)
    tile_adapter_slot = jnp.sum(
        jnp.where(tile_adapter[:, None] == adapter_ids[None, :], adapter_slot[None, :], 0), axis=1
    )
    my_lengths = lax.dynamic_slice_in_dim(tile_length, my_index * tiles_here, tiles_here)
    active_rows = (jnp.arange(TILE)[None, :] < my_lengths[:, None]).reshape(tok_count, 1)
    masked_own = cotangent * active_rows.astype(jnp.bfloat16)
    masked_full = lax.all_gather(masked_own, "mp", axis=1, tiled=True)
    sent_down = down_store[:, 0][tile_adapter_slot]
    sent_up = up_store[tile_adapter_slot]
    down_panel, up_panel = (
        lax.all_to_all(sent_down, "adapter", split_axis=0, concat_axis=1, tiled=True),
        lax.all_to_all(sent_up, "adapter", split_axis=0, concat_axis=1, tiled=True),
    )
    token_tiles = tokens.reshape(tiles_here, TILE, feat_part)
    frozen_part = jnp.dot(
        tokens,
        lax.all_gather(value_weight, "adapter", axis=1, tiled=True),
        preferred_element_type=jnp.float32,
    )
    frozen_local = lax.psum_scatter(frozen_part, "mp", scatter_dimension=1, tiled=True)
    down_part = jnp.einsum(
        "ntd,ndr->ntr", token_tiles, down_panel, preferred_element_type=jnp.float32
    )
    down_sum = lax.psum(down_part, "mp")
    down_portion = down_sum.astype(jnp.bfloat16)
    adapter_term = jnp.einsum(
        "ntr,nrv->ntv", down_portion, up_panel, preferred_element_type=jnp.float32
    ).reshape(tok_count, head_cols)
    projected = (
        (frozen_local + adapter_scale * adapter_term) * active_rows.astype(jnp.float32)
    ).astype(jnp.bfloat16)
    tile_mask = masked_own.reshape(tiles_here, TILE, head_cols)
    backward_piece = adapter_scale * jnp.einsum(
        "ntv,nrv->ntr", tile_mask, up_panel, preferred_element_type=jnp.float32
    )
    backward_portion = lax.psum(backward_piece, "mp").astype(jnp.bfloat16)
    frozen_backward = lax.dot_general(
        masked_full,
        lax.all_gather(value_weight, "adapter", axis=1, tiled=True),
        (((1,), (1,)), ((), ())),
        preferred_element_type=jnp.float32,
    )
    adapter_backward = jnp.einsum(
        "ntr,ndr->ntd", backward_portion, down_panel, preferred_element_type=jnp.float32
    ).reshape(tok_count, feat_part)
    token_gradient = (frozen_backward + adapter_backward).astype(jnp.bfloat16)
    home_down = jnp.einsum(
        "ntd,ntr->ndr", token_tiles, backward_portion, preferred_element_type=jnp.float32
    )
    local_up_weight = adapter_scale * jnp.einsum(
        "ntr,ntv->nrv", down_portion, tile_mask, preferred_element_type=jnp.float32
    )
    arrived_down, arrived_up = (
        lax.all_to_all(home_down, "adapter", split_axis=1, concat_axis=0, tiled=True),
        lax.all_to_all(local_up_weight, "adapter", split_axis=1, concat_axis=0, tiled=True),
    )
    selector = (adapter_ids[:, None] == tile_adapter_slot[None, :]).astype(jnp.float32)
    down_gradient = jnp.dot(
        selector, arrived_down.reshape(tile_total, -1), precision=lax.Precision.HIGHEST
    ).reshape(down_store.shape)
    up_gradient = jnp.dot(
        selector, arrived_up.reshape(tile_total, -1), precision=lax.Precision.HIGHEST
    ).reshape(up_store.shape)
    new_down, new_down_first, new_down_second = adam_step(
        down_store, down_first, down_second, down_gradient
    )
    new_up, new_up_first, new_up_second = adam_step(up_store, up_first, up_second, up_gradient)
    return (
        projected,
        token_gradient,
        new_down,
        new_down_first,
        new_down_second,
        new_up,
        new_up_first,
        new_up_second,
    )


def solution(mesh):
    placed = (
        P("adapter", "mp"),
        P("adapter", "mp"),
        P("mp", "adapter"),
        P(None, "mp", "adapter", None),
        P(None, "mp", "adapter", None),
        P(None, "mp", "adapter", None),
        P(None, "adapter", "mp"),
        P(None, "adapter", "mp"),
        P(None, "adapter", "mp"),
        P(),
        P(),
        P(),
    )
    return jax.shard_map(
        shards,
        mesh=mesh,
        in_specs=placed,
        out_specs=(
            P("adapter", "mp"),
            P("adapter", "mp"),
            P(None, "mp", "adapter", None),
            P(None, "mp", "adapter", None),
            P(None, "mp", "adapter", None),
            P(None, "adapter", "mp"),
            P(None, "adapter", "mp"),
            P(None, "adapter", "mp"),
        ),
        check_vma=False,
    )
```

profile of v0, /device:TPU:6, one launch (start us, length us, event | category | flops | bytes accessed | tf_op | source)
XLA Modules:
  0.0 215.0 jit_solution(986982977776494731)
XLA Ops:
  8.8 1.5 gather_fusion.1
  12.2 18.7 %all-to-all-start.1 = ((bf16[64,2,192]{2,1,0:T(2,128)(2,1)}), bf16[64,2,192]{2,1,0:T(2,128)(2,1)S(1)}, u32[]{:S(2)}, u32[]{:S(2)}) async-start(bf16[64,2,192]{2,1,0:T(2,128)(2,1)} %reshape.154), calls=%async_computation.2 | async-start | bytes 131072 | tf_op jit(solution)/shard_map/all_to_all | solution.py:60
  31.0 1.4 copy.59
  33.2 1.2 reshape.156
  34.4 11.3 %all-to-all-done.1 = bf16[64,2,192]{2,1,0:T(2,128)(2,1)S(1)} async-done(((bf16[64,2,192]{2,1,0:T(2,128)(2,1)}), bf16[64,2,192]{2,1,0:T(2,128)(2,1)S(1)}, u32[]{:S(2)}, u32[]{:S(2)}) %all-to-all-start.1) | async-done | bytes 49184 | tf_op jit(solution)/shard_map/all_to_all | solution.py:60
  45.7 4.6 %all-to-all-start = ((bf16[64,2,1536]{2,1,0:T(2,128)(2,1)}), bf16[64,2,1536]{2,1,0:T(2,128)(2,1)S(1)}, u32[]{:S(2)}, u32[]{:S(2)}) async-start(bf16[64,2,1536]{2,1,0:T(2,128)(2,1)} %reshape.156), calls=%async_computation.1 | async-start | bytes 786432 | tf_op jit(solution)/shard_map/all_to_all | solution.py:59
  51.2 25.0 %all-to-all-done = bf16[64,2,1536]{2,1,0:T(2,128)(2,1)S(1)} async-done(((bf16[64,2,1536]{2,1,0:T(2,128)(2,1)}), bf16[64,2,1536]{2,1,0:T(2,128)(2,1)S(1)}, u32[]{:S(2)}, u32[]{:S(2)}) %all-to-all-start) | async-done | bytes 393248 | tf_op jit(solution)/shard_map/all_to_all | solution.py:59
  78.2 23.0 %all-reduce.2 = (bf16[3,128,64]{1,2,0:T(8,128)(2,1)S(1)}, bf16[3,128,64]{1,2,0:T(8,128)(2,1)S(1)}) all-reduce(f32[3,128,64]{1,2,0:T(8,128)S(1)} %convolution_bitcast_fusion.1, f32[3,128,64]{1,2,0:T(8,128)S(1)} %convolution_multiply_fusion.2), channel_id=1, replica_groups=mesh['adapter'=64,'mp'=8] {'mp'}, use_global_device_ids=true, to_apply=%region_2.3 | all-reduce | flops 49152 | bytes 294912 | tf_op jit(solution)/shard_map/psum | solution.py:72
  102.1 7.4 %all-to-all-start.3 = ((f32[3,64,128]{2,0,1:T(4,128)}), f32[3,64,128]{2,0,1:T(4,128)S(1)}, u32[]{:S(2)}, u32[]{:S(2)}) async-start(f32[3,64,128]{2,0,1:T(4,128)} %copy.70), calls=%async_computation.4 | async-start | bytes 262144 | tf_op jit(solution)/shard_map/all_to_all | solution.py:103
  109.5 1.1 convolution_bitcast_fusion
  110.6 1.8 copy.65
  112.4 2.3 %reshape.158 = f32[64,1,3072]{2,1,0:T(1,128)} reshape(f32[1024,3,64]{2,1,0:T(4,128)S(1)} %bitcast.81) | data formatting | bytes 1572864
  114.7 12.4 %all-to-all-done.3 = f32[3,64,128]{2,0,1:T(4,128)S(1)} async-done(((f32[3,64,128]{2,0,1:T(4,128)}), f32[3,64,128]{2,0,1:T(4,128)S(1)}, u32[]{:S(2)}, u32[]{:S(2)}) %all-to-all-start.3) | async-done | bytes 98336 | tf_op jit(solution)/shard_map/all_to_all | solution.py:103
  127.2 6.4 %all-to-all-start.2 = ((f32[64,1,3072]{2,1,0:T(1,128)}), f32[64,1,3072]{2,1,0:T(1,128)S(1)}, u32[]{:S(2)}, u32[]{:S(2)}) async-start(f32[64,1,3072]{2,1,0:T(1,128)} %reshape.158), calls=%async_computation.3 | async-start | bytes 1572864 | tf_op jit(solution)/shard_map/all_to_all | solution.py:102
  133.6 35.3 %all-gather.2.cloned.1.call-done = bf16[1024,1024]{0,1:T(8,128)(2,1)} async-done(((bf16[1024,16]{0,1:T(8,128)(2,1)}), bf16[1024,1024]{0,1:T(8,128)(2,1)}) %all-gather.2.cloned.1.call-update) | async-done | bytes 2097168 | tf_op jit(solution)/shard_map/all_gather | solution.py:65
  169.0 3.8 %fusion.23 = f32[384,1024]{1,0:T(8,128)} fusion(bf16[384,1024]{1,0:T(8,128)(2,1)S(1)} %copy-done, bf16[1024,1024]{0,1:T(8,128)(2,1)} %all-gather.2.cloned.1.call-done), kind=kOutput, calls=%fused_computation.44 | convolution fusion | flops 805306368 | bytes 4456448 | tf_op jit(solution)/shard_map/dot_general | solution.py:63
  172.8 14.7 %all_gather.8 = bf16[384,1024]{1,0:T(8,128)(2,1)} all-gather(bf16[384,128]{1,0:T(8,128)(2,1)S(1)} %broadcast_multiply_fusion), channel_id=1, replica_groups=mesh['adapter'=64,'mp'=8] {'mp'}, dimensions={1}, use_global_device_ids=true | all-gather | bytes 884736 | tf_op jit(solution)/shard_map/all_gather | solution.py:55
  188.4 1.6 fusion.24
  190.1 1.7 divide_subtract_fusion.1
  191.8 3.9 %fusion = bf16[384,1024]{1,0:T(8,128)(2,1)} fusion(f32[3,128,1024]{2,1,0:T(8,128)} %fusion.24, bf16[384,1024]{1,0:T(8,128)(2,1)S(1)} %copy-done.5, bf16[1024,1024]{0,1:T(8,128)(2,1)} %all-gather.2.cloned.1.call-done), kind=kOutput, calls=%fused_computation.3 | convolution fusion | flops 806092800 | bytes 5242880 | tf_op jit(solution)/shard_map/dot_general | solution.py:85
  196.3 3.6 %reduce.2 = f32[64,3072]{1,0:T(8,128)} reduce(f32[64,1,3072]{2,1,0:T(1,128)S(1)} %all-to-all-done.2, f32[]{:T(128)} %broadcast.78), dimensions={1}, to_apply=%all_to_all.56.reduce_sub_computation | reduce | bytes 1572868 | tf_op jit(solution)/shard_map/all_to_all | solution.py:102
  199.8 2.3 %reshape.159 = f32[1024,3,64]{2,1,0:T(4,128)S(1)} reshape(f32[64,3072]{1,0:T(8,128)} %reduce.2) | data formatting | bytes 1572864
  203.8 2.6 %divide_subtract_fusion = (f32[128,1,16,64]{0,3,2,1:T(8,128)}, f32[128,1,16,64]{0,3,2,1:T(8,128)}, f32[128,1,16,64]{0,3,2,1:T(8,128)}) fusion(bf16[128,1,16,64]{0,3,2,1:T(8,128)(2,1)S(1)} %copy-done.4, f32[128,1,16,64]{0,3,2,1:T(8,128)S(1)} %bitcast.88, f32[128,1,16,64]{0,3,2,1:T(8,128)} %param.16, f32[128,1,16,64]{0,3,2,1:T(8,128)} %param.17), kind=kLoop, calls=%fused_computation.11 | loop fusion | flops 1703936 | bytes 3407872 | tf_op jit(solution)/shard_map/sub | solution.py:22
  206.4 1.7 fusion.3
  (52 shorter events, 11.2 us)
Async XLA Ops:
  7.2 69.7 %copy-start = (bf16[384,1024]{1,0:T(8,128)(2,1)S(1)}, bf16[384,1024]{1,0:T(8,128)(2,1)}, u32[]{:S(2)}) copy-start(bf16[384,1024]{1,0:T(8,128)(2,1)} %param.12) | copy-start | bytes 2359300
  7.2 161.8 %all-gather.2.cloned.1.call-start = ((), (), s32[]{:S(2)}) async-start(), calls=%async_computation.5 | async-start | bytes 2129920 | tf_op jit(solution)/shard_map/all_gather | solution.py:65
  12.2 33.5 %all-to-all-start.1 = ((bf16[64,2,192]{2,1,0:T(2,128)(2,1)}), bf16[64,2,192]{2,1,0:T(2,128)(2,1)S(1)}, u32[]{:S(2)}, u32[]{:S(2)}) async-start(bf16[64,2,192]{2,1,0:T(2,128)(2,1)} %reshape.154), calls=%async_computation.2 | async-start | bytes 131072 | tf_op jit(solution)/shard_map/all_to_all | solution.py:60
  30.9 19.4 %copy-start.9 = (s32[192]{0:T(256)S(1)}, s32[192]{0:T(256)}, u32[]{:S(2)}) copy-start(s32[192]{0:T(256)} %param.22) | copy-start | bytes 2308
  30.9 19.5 %copy-start.7 = (bf16[384,128]{1,0:T(8,128)(2,1)S(1)}, bf16[384,128]{1,0:T(8,128)(2,1)}, u32[]{:S(2)}) copy-start(bf16[384,128]{1,0:T(8,128)(2,1)} %param.13) | copy-start | bytes 294916
  45.7 30.6 %all-to-all-start = ((bf16[64,2,1536]{2,1,0:T(2,128)(2,1)}), bf16[64,2,1536]{2,1,0:T(2,128)(2,1)S(1)}, u32[]{:S(2)}, u32[]{:S(2)}) async-start(bf16[64,2,1536]{2,1,0:T(2,128)(2,1)} %reshape.156), calls=%async_computation.1 | async-start | bytes 786432 | tf_op jit(solution)/shard_map/all_to_all | solution.py:59
  76.9 0.9 copy-start.1
  102.1 25.1 %all-to-all-start.3 = ((f32[3,64,128]{2,0,1:T(4,128)}), f32[3,64,128]{2,0,1:T(4,128)S(1)}, u32[]{:S(2)}, u32[]{:S(2)}) async-start(f32[3,64,128]{2,0,1:T(4,128)} %copy.70), calls=%async_computation.4 | async-start | bytes 262144 | tf_op jit(solution)/shard_map/all_to_all | solution.py:103
  127.2 68.6 %all-to-all-start.2 = ((f32[64,1,3072]{2,1,0:T(1,128)}), f32[64,1,3072]{2,1,0:T(1,128)S(1)}, u32[]{:S(2)}, u32[]{:S(2)}) async-start(f32[64,1,3072]{2,1,0:T(1,128)} %reshape.158), calls=%async_computation.3 | async-start | bytes 1572864 | tf_op jit(solution)/shard_map/all_to_all | solution.py:102
  133.6 72.8 %reduce-scatter.2.cloned.1.call-start = ((), (), s32[]{:S(2)}) async-start(), calls=%async_computation.6 | async-start | bytes 1769472 | tf_op jit(solution)/shard_map/reduce_scatter | solution.py:68
  172.8 15.7 %copy-start.2 = (bf16[3,64,16,64]{3,2,1,0:T(8,128)(2,1)S(1)}, bf16[3,64,16,64]{3,2,1,0:T(8,128)(2,1)}, u32[]{:S(2)}) copy-start(bf16[3,64,16,64]{3,2,1,0:T(8,128)(2,1)} %copy-done.1) | copy-start | bytes 1179652
  172.8 17.3 %copy-start.3 = (bf16[128,1,128]{2,0,1:T(8,128)(2,1)S(1)}, bf16[128,1,128]{2,0,1:T(8,128)(2,1)}, u32[]{:S(2)}) copy-start(bf16[128,1,128]{2,0,1:T(8,128)(2,1)} %param.18) | copy-start | bytes 98308
  172.8 17.3 %copy-start.8 = (f32[128,1,128]{2,1,0:T(1,128)S(1)}, f32[128,1,128]{2,1,0:T(1,128)}, u32[]{:S(2)}) copy-start(f32[128,1,128]{2,1,0:T(1,128)} %param.19) | copy-start | bytes 196612
  187.5 4.3 %copy-start.5 = (bf16[384,1024]{1,0:T(8,128)(2,1)S(1)}, bf16[384,1024]{1,0:T(8,128)(2,1)}, u32[]{:S(2)}) copy-start(bf16[384,1024]{1,0:T(8,128)(2,1)} %all_gather.8) | copy-start | bytes 2359300
  202.3 1.5 copy-start.4
  202.8 3.7 %copy-start.6 = (f32[3,128,128]{2,1,0:T(8,128)S(1)}, f32[3,128,128]{2,1,0:T(8,128)}, u32[]{:S(2)}) copy-start(f32[3,128,128]{2,1,0:T(8,128)} %convolution_multiply_fusion) | copy-start | bytes 589828
Sparse Core Ops, SparseCore 0:
  10.9 157.9 all-gather.1
  172.9 31.3 reduce-scatter.1
where the time goes:
time: 217 us; the launch traced here: 215 us
  waiting for transfers between devices  84.7 us (39%)
  blocking collectives  37.7 us (17%)
  starting transfers between devices  37.3 us (17%)
  local copies, waits for them, and re-layouts  16.2 us (7%)
  matrix products  14.8 us (7%)
  between operations  14.3 us (7%)
  other arithmetic  9.87 us (5%)
    all_gather x1, waiting for transfers between devices, shards(): lax.all_gather(value_weight, 'adapter', axis=1, tiled=True)  35.3 us
    all_to_all x1, waiting for transfers between devices, shards(): lax.all_to_all(sent_down, 'adapter', split_axis=0, concat_axis=1, tiled=T...  25 us
    psum x1, blocking collectives, shards(): down_sum = lax.psum(down_part, 'mp')  23 us
    all_to_all x1, starting transfers between devices, shards(): lax.all_to_all(sent_up, 'adapter', split_axis=0, concat_axis=1, tiled=True)  18.7 us
    all_gather x1, blocking collectives, shards(): masked_full = lax.all_gather(masked_own, 'mp', axis=1, tiled=True)  14.7 us
    all_to_all x1, waiting for transfers between devices, shards(): lax.all_to_all(local_up_weight, 'adapter', split_axis=1, concat_axis=0, t...  12.4 us
    all_to_all x1, waiting for transfers between devices, shards(): lax.all_to_all(sent_up, 'adapter', split_axis=0, concat_axis=1, tiled=True)  11.3 us
    unnamed x27, local copies, waits for them, and re-layouts  9.48 us
  transfers between devices with their start and end apart: 6, of which 4 were waited for; matrix products, arithmetic and copies ran while one was open for 18% of the time, Pallas kernels for 0%

commit v1 on v0

--- a/solution.py
+++ b/solution.py
@@ -1,7 +1,7 @@
 import jax
 import jax.numpy as jnp
 from jax import lax
-from jax.sharding import PartitionSpec as P
+from jax.sharding import Mesh, PartitionSpec as P
 
 TILE = 128
 STEP = 100
@@ -25,6 +25,26 @@
     return (moved, new_first, new_second)
 
 
+ADAPTER = ("ay", "az")
+
+
+def gather_weight(value_weight):
+    first = lax.all_gather(value_weight, "az", axis=1, tiled=True)
+    return lax.all_gather(first, "ay", axis=1, tiled=True)
+
+
+def split_adapter(mesh):
+    devices = mesh.devices
+    n_adapter = devices.shape[0]
+    try:
+        n_y = len({d.coords[1] for d in devices[:, 0]})
+    except (AttributeError, IndexError, TypeError):
+        n_y = 1
+    if n_y < 1 or n_adapter % n_y:
+        n_y = 1
+    return Mesh(devices.reshape(n_y, n_adapter // n_y, devices.shape[1]), ("ay", "az", "mp"))
+
+
 def shards(
     tokens,
     cotangent,
@@ -44,7 +64,7 @@
     head_cols = cotangent.shape[1]
     tiles_here = tok_count // TILE
     adapter_count = adapter_slot.shape[0]
-    my_index = lax.axis_index("adapter")
+    my_index = lax.axis_index(ADAPTER)
     adapter_ids = jnp.arange(adapter_count, dtype=jnp.int32)
     tile_adapter_slot = jnp.sum(
         jnp.where(tile_adapter[:, None] == adapter_ids[None, :], adapter_slot[None, :], 0), axis=1
@@ -53,16 +73,26 @@
     active_rows = (jnp.arange(TILE)[None, :] < my_lengths[:, None]).reshape(tok_count, 1)
     masked_own = cotangent * active_rows.astype(jnp.bfloat16)
     masked_full = lax.all_gather(masked_own, "mp", axis=1, tiled=True)
-    sent_down = down_store[:, 0][tile_adapter_slot]
-    sent_up = up_store[tile_adapter_slot]
-    down_panel, up_panel = (
-        lax.all_to_all(sent_down, "adapter", split_axis=0, concat_axis=1, tiled=True),
-        lax.all_to_all(sent_up, "adapter", split_axis=0, concat_axis=1, tiled=True),
+    n_adapter = tile_total // tiles_here
+    row_part = down_store.shape[2]
+    rank = down_store.shape[3]
+    sent_down = down_store[:, 0][tile_adapter_slot].reshape(tile_total, row_part * rank)
+    sent_up = up_store[tile_adapter_slot].reshape(tile_total, head_cols)
+    sent = jnp.concatenate([sent_down, sent_up], axis=1)
+    arrived = lax.all_to_all(sent, ADAPTER, split_axis=0, concat_axis=0, tiled=True)
+    arrived = arrived.reshape(n_adapter, tiles_here, row_part * rank + head_cols)
+    down_panel = (
+        arrived[:, :, : row_part * rank]
+        .reshape(n_adapter, tiles_here, row_part, rank)
+        .transpose(1, 0, 2, 3)
+        .reshape(tiles_here, n_adapter * row_part, rank)
     )
+    up_panel = arrived[:, :, row_part * rank :].transpose(1, 0, 2)
+    w_full = gather_weight(value_weight)
     token_tiles = tokens.reshape(tiles_here, TILE, feat_part)
     frozen_part = jnp.dot(
         tokens,
-        lax.all_gather(value_weight, "adapter", axis=1, tiled=True),
+        w_full,
         preferred_element_type=jnp.float32,
     )
     frozen_local = lax.psum_scatter(frozen_part, "mp", scatter_dimension=1, tiled=True)
@@ -84,7 +114,7 @@
     backward_portion = lax.psum(backward_piece, "mp").astype(jnp.bfloat16)
     frozen_backward = lax.dot_general(
         masked_full,
-        lax.all_gather(value_weight, "adapter", axis=1, tiled=True),
+        w_full,
         (((1,), (1,)), ((), ())),
         preferred_element_type=jnp.float32,
     )
@@ -98,10 +128,12 @@
     local_up_weight = adapter_scale * jnp.einsum(
         "ntr,ntv->nrv", down_portion, tile_mask, preferred_element_type=jnp.float32
     )
-    arrived_down, arrived_up = (
-        lax.all_to_all(home_down, "adapter", split_axis=1, concat_axis=0, tiled=True),
-        lax.all_to_all(local_up_weight, "adapter", split_axis=1, concat_axis=0, tiled=True),
+    grads = jnp.concatenate(
+        [home_down.reshape(tiles_here, n_adapter, row_part * rank), local_up_weight], axis=2
     )
+    grads = lax.all_to_all(grads, ADAPTER, split_axis=1, concat_axis=0, tiled=True)
+    arrived_down = grads[:, 0, : row_part * rank]
+    arrived_up = grads[:, 0, row_part * rank :]
     selector = (adapter_ids[:, None] == tile_adapter_slot[None, :]).astype(jnp.float32)
     down_gradient = jnp.dot(
         selector, arrived_down.reshape(tile_total, -1), precision=lax.Precision.HIGHEST
@@ -126,16 +158,17 @@
 
 
 def solution(mesh):
+    mesh = split_adapter(mesh)
     placed = (
-        P("adapter", "mp"),
-        P("adapter", "mp"),
-        P("mp", "adapter"),
-        P(None, "mp", "adapter", None),
-        P(None, "mp", "adapter", None),
-        P(None, "mp", "adapter", None),
-        P(None, "adapter", "mp"),
-        P(None, "adapter", "mp"),
-        P(None, "adapter", "mp"),
+        P(ADAPTER, "mp"),
+        P(ADAPTER, "mp"),
+        P("mp", ADAPTER),
+        P(None, "mp", ADAPTER, None),
+        P(None, "mp", ADAPTER, None),
+        P(None, "mp", ADAPTER, None),
+        P(None, ADAPTER, "mp"),
+        P(None, ADAPTER, "mp"),
+        P(None, ADAPTER, "mp"),
         P(),
         P(),
         P(),
@@ -145,14 +178,14 @@
         mesh=mesh,
         in_specs=placed,
         out_specs=(
-            P("adapter", "mp"),
-            P("adapter", "mp"),
-            P(None, "mp", "adapter", None),
-            P(None, "mp", "adapter", None),
-            P(None, "mp", "adapter", None),
-            P(None, "adapter", "mp"),
-            P(None, "adapter", "mp"),
-            P(None, "adapter", "mp"),
+            P(ADAPTER, "mp"),
+            P(ADAPTER, "mp"),
+            P(None, "mp", ADAPTER, None),
+            P(None, "mp", ADAPTER, None),
+            P(None, "mp", ADAPTER, None),
+            P(None, ADAPTER, "mp"),
+            P(None, ADAPTER, "mp"),
+            P(None, ADAPTER, "mp"),
         ),
         check_vma=False,
     )

time: 217 us -> 209 us (0.963)
  blocking collectives: 37.7 us -> 93 us
  waiting for transfers between devices: 84.7 us -> 39.5 us
  starting transfers between devices: 37.3 us -> 32.5 us
  matrix products: 14.8 us -> 10.1 us
  local copies, waits for them, and re-layouts: 16.2 us -> 12.6 us
  other arithmetic: 9.87 us -> 6.53 us
    all_gather x0 -> x1, blocking collectives: none -> 55.8 us  [gather_weight(): first = lax.all_gather(value_weight, 'az', axis=1, tiled=True)]
    all_gather x1, waiting for transfers between devices: 35.3 us -> 0.02 us  [gather_weight(): return lax.all_gather(first, 'ay', axis=1, tiled=True)]
    all_to_all x4 -> x2, waiting for transfers between devices: 48.7 us -> 39.4 us  [the longest x1 39.4 us: shards(): lax.all_to_all(grads, ADAPTER, split_axis=1, concat_axis=0, tiled=True)]
    unnamed x27 -> x23, local copies, waits for them, and re-layouts: 9.48 us -> 1.43 us
    all_to_all x4 -> x2, starting transfers between devices: 37.2 us -> 32.4 us  [the longest x1 18.7 us: shards(): lax.all_to_all(sent, ADAPTER, split_axis=0, concat_axis=0, tiled=True)]
    all_to_all x2 -> x0, other arithmetic: 3.85 us -> none  [the longest x1 3.58 us: shards(): lax.all_to_all(home_down, 'adapter', split_axis=1, concat_axis=0, tiled=T...]
    concatenate x0 -> x2, other arithmetic: none -> 2.32 us  [the longest x1 1.23 us: shards(): jnp.concatenate([home_down.reshape(tiles_here, n_adapter, row_part * rank...]
    concatenate x0 -> x3, local copies, waits for them, and re-layouts: none -> 2.2 us  [the longest x1 1.64 us: shards(): jnp.concatenate([home_down.reshape(tiles_here, n_adapter, row_part * rank...]
  transfers between devices with their start and end apart: 6 -> 4, of which waited for: 4 -> 1; matrix products, arithmetic and copies ran while one was open for 18% -> 9% of each run, Pallas kernels for 0% -> 0%
where the time goes in v1:
time: 209 us
  blocking collectives  93 us (44%)
  waiting for transfers between devices  39.5 us (19%)
  starting transfers between devices  32.5 us (16%)
  between operations  14.3 us (7%)
  local copies, waits for them, and re-layouts  12.6 us (6%)
  matrix products  10.1 us (5%)
  other arithmetic  6.53 us (3%)
    all_gather x1, blocking collectives, gather_weight(): first = lax.all_gather(value_weight, 'az', axis=1, tiled=True)  55.8 us
    all_to_all x1, waiting for transfers between devices, shards(): lax.all_to_all(grads, ADAPTER, split_axis=1, concat_axis=0, tiled=True)  39.4 us
    psum x1, blocking collectives, shards(): down_sum = lax.psum(down_part, 'mp')  22.8 us
    all_to_all x1, starting transfers between devices, shards(): lax.all_to_all(sent, ADAPTER, split_axis=0, concat_axis=0, tiled=True)  18.7 us
    all_gather x1, blocking collectives, shards(): masked_full = lax.all_gather(masked_own, 'mp', axis=1, tiled=True)  14.3 us
    all_to_all x1, starting transfers between devices, shards(): lax.all_to_all(grads, ADAPTER, split_axis=1, concat_axis=0, tiled=True)  13.6 us
  transfers between devices with their start and end apart: 4, of which 1 were waited for; matrix products, arithmetic and copies ran while one was open for 9% of the time, Pallas kernels for 0%

profile of v1, /device:TPU:6, one launch (start us, length us, event | category | flops | bytes accessed | tf_op | source)
XLA Modules:
  0.0 208.6 jit_solution(10256265634116957441)
XLA Ops:
  7.2 0.9 select_reduce_fusion
  8.2 1.5 gather_fusion.1
  9.7 1.4 copy.68
  11.0 0.8 gather_fusion
  12.4 1.1 pad_maximum_fusion.1
  13.5 18.7 %all-to-all-start = ((bf16[64,3,1152]{2,1,0:T(4,128)(2,1)}), bf16[64,3,1152]{2,1,0:T(4,128)(2,1)S(1)}, u32[]{:S(2)}, u32[]{:S(2)}) async-start(bf16[64,3,1152]{2,1,0:T(4,128)(2,1)} %pad_maximum_fusion.1), calls=%async_computation.1 | async-start | bytes 1179648 | tf_op jit(solution)/shard_map/all_to_all | solution.py:82
  32.3 55.8 %all_gather.9 = bf16[1024,256]{0,1:T(8,128)(2,1)} all-gather(bf16[1024,16]{0,1:T(8,128)(2,1)S(1)} %copy-done.6), channel_id=1, replica_groups=mesh['ay'=4,'az'=16,'mp'=8] {'az'}, dimensions={1}, use_global_device_ids=true | all-gather | bytes 557056 | tf_op jit(solution)/shard_map/all_gather | solution.py:32
  90.0 22.8 %all-reduce.2 = (bf16[3,128,64]{1,2,0:T(8,128)(2,1)S(1)}, bf16[3,128,64]{1,2,0:T(8,128)(2,1)S(1)}) all-reduce(f32[3,128,64]{1,2,0:T(8,128)S(1)} %convolution_bitcast_fusion.1, f32[3,128,64]{1,2,0:T(8,128)S(1)} %convolution_multiply_fusion.2), channel_id=1, replica_groups=mesh['ay'=4,'az'=16,'mp'=8] {'mp'}, use_global_device_ids=true, to_apply=%region_2.3 | all-reduce | flops 49152 | bytes 294912 | tf_op jit(solution)/shard_map/psum | solution.py:102
  112.8 1.1 convolution_bitcast_fusion
  113.9 1.6 copy.73
  115.5 1.3 reshape.143
  117.0 1.2 pad_maximum_fusion
  118.3 1.6 copy.74
  119.9 13.6 %all-to-all-start.1 = ((f32[3,64,1152]{2,0,1:T(4,128)}), f32[3,64,1152]{2,0,1:T(4,128)S(1)}, u32[]{:S(2)}, u32[]{:S(2)}) async-start(f32[3,64,1152]{2,0,1:T(4,128)} %copy.74), calls=%async_computation.2 | async-start | bytes 2359296 | tf_op jit(solution)/shard_map/all_to_all | solution.py:134
  133.6 3.7 %fusion.21 = f32[384,1024]{1,0:T(8,128)} fusion(bf16[384,1024]{1,0:T(8,128)(2,1)S(1)} %copy-done, bf16[1024,1024]{0,1:T(8,128)(2,1)} %all-gather.2.cloned.1.call-done), kind=kOutput, calls=%fused_computation.45 | convolution fusion | flops 805306368 | bytes 4456448 | tf_op jit(solution)/shard_map/dot_general | solution.py:93
  137.4 14.3 %all_gather.11 = bf16[384,1024]{1,0:T(8,128)(2,1)S(1)} all-gather(bf16[384,128]{1,0:T(8,128)(2,1)S(1)} %broadcast_multiply_fusion), channel_id=1, replica_groups=mesh['ay'=4,'az'=16,'mp'=8] {'mp'}, dimensions={1}, use_global_device_ids=true | all-gather | bytes 884736 | tf_op jit(solution)/shard_map/all_gather | solution.py:75
  152.4 1.9 fusion
  154.3 39.4 %all-to-all-done.1 = f32[3,64,1152]{2,0,1:T(4,128)S(1)} async-done(((f32[3,64,1152]{2,0,1:T(4,128)}), f32[3,64,1152]{2,0,1:T(4,128)S(1)}, u32[]{:S(2)}, u32[]{:S(2)}) %all-to-all-start.1) | async-done | bytes 884768 | tf_op jit(solution)/shard_map/all_to_all | solution.py:134
  193.8 2.0 all_to_all.21
  195.8 0.8 slice-done.1
  196.7 0.9 divide_subtract_fusion.1
  197.6 1.0 fusion.1
  198.6 1.4 divide_subtract_fusion
  200.0 1.7 fusion.6
  (48 shorter events, 3.3 us)
Async XLA Ops:
  7.2 82.1 %copy-start = (bf16[384,1024]{1,0:T(8,128)(2,1)S(1)}, bf16[384,1024]{1,0:T(8,128)(2,1)}, u32[]{:S(2)}) copy-start(bf16[384,1024]{1,0:T(8,128)(2,1)} %param.12) | copy-start | bytes 2359300
  11.8 20.4 %copy-start.6 = (bf16[1024,16]{0,1:T(8,128)(2,1)S(1)}, bf16[1024,16]{0,1:T(8,128)(2,1)}, u32[]{:S(2)}) copy-start(bf16[1024,16]{0,1:T(8,128)(2,1)} %param.14) | copy-start | bytes 98308
  12.4 75.8 %copy-start.10 = (s32[192]{0:T(256)S(1)}, s32[192]{0:T(256)}, u32[]{:S(2)}) copy-start(s32[192]{0:T(256)} %param.22) | copy-start | bytes 2308
  12.4 75.9 %copy-start.5 = (bf16[384,128]{1,0:T(8,128)(2,1)S(1)}, bf16[384,128]{1,0:T(8,128)(2,1)}, u32[]{:S(2)}) copy-start(bf16[384,128]{1,0:T(8,128)(2,1)} %param.13) | copy-start | bytes 294916
  13.5 75.0 %all-to-all-start = ((bf16[64,3,1152]{2,1,0:T(4,128)(2,1)}), bf16[64,3,1152]{2,1,0:T(4,128)(2,1)S(1)}, u32[]{:S(2)}, u32[]{:S(2)}) async-start(bf16[64,3,1152]{2,1,0:T(4,128)(2,1)} %pad_maximum_fusion.1), calls=%async_computation.1 | async-start | bytes 1179648 | tf_op jit(solution)/shard_map/all_to_all | solution.py:82
  32.2 101.4 %all-gather.2.cloned.1.call-start = ((), (), s32[]{:S(2)}) async-start(), calls=%async_computation.3 | async-start | bytes 2621440 | tf_op jit(solution)/shard_map/all_gather | solution.py:33
  119.9 73.8 %all-to-all-start.1 = ((f32[3,64,1152]{2,0,1:T(4,128)}), f32[3,64,1152]{2,0,1:T(4,128)S(1)}, u32[]{:S(2)}, u32[]{:S(2)}) async-start(f32[3,64,1152]{2,0,1:T(4,128)} %copy.74), calls=%async_computation.2 | async-start | bytes 2359296 | tf_op jit(solution)/shard_map/all_to_all | solution.py:134
  133.6 66.5 %reduce-scatter.2.cloned.1.call-start = ((), (), s32[]{:S(2)}) async-start(), calls=%async_computation.4 | async-start | bytes 1769472 | tf_op jit(solution)/shard_map/reduce_scatter | solution.py:98
  137.4 15.0 %copy-start.7 = (bf16[1024,1024]{0,1:T(8,128)(2,1)S(1)}, bf16[1024,1024]{0,1:T(8,128)(2,1)}, u32[]{:S(2)}) copy-start(bf16[1024,1024]{0,1:T(8,128)(2,1)} %all-gather.2.cloned.1.call-done) | copy-start | bytes 6291460
  193.7 2.1 copy-start.1
  193.7 2.1 copy-start.8
  193.7 2.1 %copy-start.9 = (f32[128,1,128]{2,1,0:T(1,128)S(1)}, f32[128,1,128]{2,1,0:T(1,128)}, u32[]{:S(2)}) copy-start(f32[128,1,128]{2,1,0:T(1,128)} %param.20) | copy-start | bytes 196612
  195.8 0.9 slice-start.1
  195.8 1.8 slice-start
  195.8 2.8 %copy-start.2 = (bf16[128,1,16,64]{0,3,2,1:T(8,128)(2,1)S(1)}, bf16[128,1,16,64]{0,3,2,1:T(8,128)(2,1)}, u32[]{:S(2)}) copy-start(bf16[128,1,16,64]{0,3,2,1:T(8,128)(2,1)} %param.15) | copy-start | bytes 786436
  195.8 2.8 %copy-start.3 = (f32[128,1,16,64]{0,3,2,1:T(8,128)S(1)}, f32[128,1,16,64]{0,3,2,1:T(8,128)}, u32[]{:S(2)}) copy-start(f32[128,1,16,64]{0,3,2,1:T(8,128)} %param.16) | copy-start | bytes 1572868
  195.8 2.8 %copy-start.4 = (f32[128,1,16,64]{0,3,2,1:T(8,128)S(1)}, f32[128,1,16,64]{0,3,2,1:T(8,128)}, u32[]{:S(2)}) copy-start(f32[128,1,16,64]{0,3,2,1:T(8,128)} %param.17) | copy-start | bytes 1572868
Sparse Core Ops, SparseCore 0:
  88.3 37.9 all-gather.1
  137.5 39.3 reduce-scatter.1

commit v2 on v1

--- a/solution.py
+++ b/solution.py
@@ -29,7 +29,11 @@
 
 
 def gather_weight(value_weight):
-    first = lax.all_gather(value_weight, "az", axis=1, tiled=True)
+    n_z = lax.axis_size("az")
+    rows, cols = value_weight.shape
+    copies = jnp.broadcast_to(value_weight.T[None], (n_z, cols, rows))
+    first = lax.all_to_all(copies, "az", split_axis=0, concat_axis=0, tiled=True)
+    first = first.reshape(n_z * cols, rows).T
     return lax.all_gather(first, "ay", axis=1, tiled=True)
 
 

time: 209 us -> 215 us (1.029)
  waiting for transfers between devices: 39.5 us -> 98.9 us
  blocking collectives: 93 us -> 37.7 us
    all_gather x1 -> x0, blocking collectives: 55.8 us -> none  [gather_weight(): first = lax.all_gather(value_weight, 'az', axis=1, tiled=True)]
    all_to_all x1, waiting for transfers between devices: 0.01 us -> 33.6 us  [shards(): lax.all_to_all(sent, ADAPTER, split_axis=0, concat_axis=0, tiled=True)]
    all_to_all x0 -> x1, waiting for transfers between devices: none -> 25.1 us  [gather_weight(): lax.all_to_all(copies, 'az', split_axis=0, concat_axis=0, tiled=True)]
    all_to_all x0 -> x1, starting transfers between devices: none -> 15.2 us  [gather_weight(): lax.all_to_all(copies, 'az', split_axis=0, concat_axis=0, tiled=True)]
    all_to_all x1, starting transfers between devices: 18.7 us -> 9.86 us  [shards(): lax.all_to_all(sent, ADAPTER, split_axis=0, concat_axis=0, tiled=True)]
    all_to_all x1, starting transfers between devices: 13.6 us -> 8.22 us  [shards(): lax.all_to_all(grads, ADAPTER, split_axis=1, concat_axis=0, tiled=True)]
  transfers between devices with their start and end apart: 4 -> 5, of which waited for: 1 -> 3; matrix products, arithmetic and copies ran while one was open for 9% -> 11% of each run, Pallas kernels for 0% -> 0%
where the time goes in v2:
time: 215 us; the launch traced here: 214 us
  waiting for transfers between devices  98.9 us (46%)
  blocking collectives  37.7 us (18%)
  starting transfers between devices  33.4 us (16%)
  between operations  14.4 us (7%)
  local copies, waits for them, and re-layouts  13.3 us (6%)
  matrix products  10.9 us (5%)
  other arithmetic  5.75 us (3%)
    all_to_all x1, waiting for transfers between devices, shards(): lax.all_to_all(grads, ADAPTER, split_axis=1, concat_axis=0, tiled=True)  39.4 us
    all_to_all x1, waiting for transfers between devices, shards(): lax.all_to_all(sent, ADAPTER, split_axis=0, concat_axis=0, tiled=True)  33.6 us
    all_to_all x1, waiting for transfers between devices, gather_weight(): lax.all_to_all(copies, 'az', split_axis=0, concat_axis=0, tiled=True)  25.1 us
    psum x1, blocking collectives, shards(): down_sum = lax.psum(down_part, 'mp')  23.4 us
    all_to_all x1, starting transfers between devices, gather_weight(): lax.all_to_all(copies, 'az', split_axis=0, concat_axis=0, tiled=True)  15.2 us
    all_gather x1, blocking collectives, shards(): masked_full = lax.all_gather(masked_own, 'mp', axis=1, tiled=True)  14.3 us
    all_to_all x1, starting transfers between devices, shards(): lax.all_to_all(sent, ADAPTER, split_axis=0, concat_axis=0, tiled=True)  9.86 us
    all_to_all x1, starting transfers between devices, shards(): lax.all_to_all(grads, ADAPTER, split_axis=1, concat_axis=0, tiled=True)  8.22 us
  transfers between devices with their start and end apart: 5, of which 3 were waited for; matrix products, arithmetic and copies ran while one was open for 11% of the time, Pallas kernels for 0%

profile of v2, /device:TPU:6, one launch (start us, length us, event | category | flops | bytes accessed | tf_op | source)
XLA Modules:
  0.0 214.3 jit_solution(1976343467458497086)
XLA Ops:
  7.2 1.7 broadcast_in_dim.14
  8.9 15.2 %all-to-all-start = ((bf16[16,16,1024]{2,1,0:T(8,128)(2,1)}), bf16[16,16,1024]{2,1,0:T(8,128)(2,1)S(1)}, u32[]{:S(2)}, u32[]{:S(2)}) async-start(bf16[16,16,1024]{2,1,0:T(8,128)(2,1)} %broadcast_in_dim.14), calls=%async_computation | async-start | bytes 1048576 | tf_op jit(solution)/shard_map/all_to_all | solution.py:35
  27.0 1.1 pad_maximum_fusion.1
  28.1 25.1 %all-to-all-done = bf16[16,16,1024]{2,1,0:T(8,128)(2,1)S(1)} async-done(((bf16[16,16,1024]{2,1,0:T(8,128)(2,1)}), bf16[16,16,1024]{2,1,0:T(8,128)(2,1)S(1)}, u32[]{:S(2)}, u32[]{:S(2)}) %all-to-all-start) | async-done | bytes 524320 | tf_op jit(solution)/shard_map/all_to_all | solution.py:35
  53.2 9.9 %all-to-all-start.1 = ((bf16[64,3,1152]{2,1,0:T(4,128)(2,1)}), bf16[64,3,1152]{2,1,0:T(4,128)(2,1)S(1)}, u32[]{:S(2)}, u32[]{:S(2)}) async-start(bf16[64,3,1152]{2,1,0:T(4,128)(2,1)} %pad_maximum_fusion.1), calls=%async_computation.2 | async-start | bytes 1179648 | tf_op jit(solution)/shard_map/all_to_all | solution.py:86
  64.1 33.6 %all-to-all-done.1 = bf16[64,3,1152]{2,1,0:T(4,128)(2,1)S(1)} async-done(((bf16[64,3,1152]{2,1,0:T(4,128)(2,1)}), bf16[64,3,1152]{2,1,0:T(4,128)(2,1)S(1)}, u32[]{:S(2)}, u32[]{:S(2)}) %all-to-all-start.1) | async-done | bytes 442400 | tf_op jit(solution)/shard_map/all_to_all | solution.py:86
  99.2 23.4 %all-reduce.2 = (bf16[3,128,64]{1,2,0:T(8,128)(2,1)}, bf16[3,128,64]{1,2,0:T(8,128)(2,1)S(1)}) all-reduce(f32[3,128,64]{1,2,0:T(8,128)S(1)} %convolution_bitcast_fusion.1, f32[3,128,64]{1,2,0:T(8,128)S(1)} %convolution_multiply_fusion.2), channel_id=1, replica_groups=mesh['ay'=4,'az'=16,'mp'=8] {'mp'}, use_global_device_ids=true, to_apply=%region_2.3 | all-reduce | flops 49152 | bytes 294912 | tf_op jit(solution)/shard_map/psum | solution.py:106
  123.2 1.1 convolution_bitcast_fusion
  124.3 1.6 copy.73
  125.9 1.3 reshape.148
  127.3 0.9 convolution_multiply_fusion.1
  128.2 1.2 pad_maximum_fusion
  129.4 1.6 copy.74
  131.1 8.2 %all-to-all-start.2 = ((f32[3,64,1152]{2,0,1:T(4,128)}), f32[3,64,1152]{2,0,1:T(4,128)S(1)}, u32[]{:S(2)}, u32[]{:S(2)}) async-start(f32[3,64,1152]{2,0,1:T(4,128)} %copy.74), calls=%async_computation.3 | async-start | bytes 2359296 | tf_op jit(solution)/shard_map/all_to_all | solution.py:138
  139.4 3.7 %fusion.21 = f32[384,1024]{1,0:T(8,128)} fusion(bf16[384,1024]{1,0:T(8,128)(2,1)S(1)} %copy-done, bf16[1024,1024]{0,1:T(8,128)(2,1)} %all-gather.2.cloned.1.call-done), kind=kOutput, calls=%fused_computation.45 | convolution fusion | flops 805306368 | bytes 4456448 | tf_op jit(solution)/shard_map/dot_general | solution.py:97
  143.1 14.3 %all_gather.7 = bf16[384,1024]{1,0:T(8,128)(2,1)S(1)} all-gather(bf16[384,128]{1,0:T(8,128)(2,1)S(1)} %broadcast_multiply_fusion), channel_id=1, replica_groups=mesh['ay'=4,'az'=16,'mp'=8] {'mp'}, dimensions={1}, use_global_device_ids=true | all-gather | bytes 884736 | tf_op jit(solution)/shard_map/all_gather | solution.py:79
  158.2 1.9 fusion
  160.1 39.4 %all-to-all-done.2 = f32[3,64,1152]{2,0,1:T(4,128)S(1)} async-done(((f32[3,64,1152]{2,0,1:T(4,128)}), f32[3,64,1152]{2,0,1:T(4,128)S(1)}, u32[]{:S(2)}, u32[]{:S(2)}) %all-to-all-start.2) | async-done | bytes 884768 | tf_op jit(solution)/shard_map/all_to_all | solution.py:138
  199.5 2.0 all_to_all.25
  201.6 0.9 slice-done.1
  202.4 0.9 divide_subtract_fusion.1
  203.3 1.0 fusion.1
  204.4 1.4 divide_subtract_fusion
  205.8 1.7 fusion.6
  (64 shorter events, 6.6 us)
Async XLA Ops:
  7.2 91.4 %copy-start = (bf16[384,1024]{1,0:T(8,128)(2,1)S(1)}, bf16[384,1024]{1,0:T(8,128)(2,1)}, u32[]{:S(2)}) copy-start(bf16[384,1024]{1,0:T(8,128)(2,1)} %param.12) | copy-start | bytes 2359300
  7.2 16.9 %copy-start.13 = (s32[128]{0:T(128)S(1)}, s32[128]{0:T(128)}, u32[]{:S(2)}) copy-start(s32[128]{0:T(128)} %param.23) | copy-start | bytes 1540
  7.2 16.9 %copy-start.12 = (s32[192]{0:T(256)S(1)}, s32[192]{0:T(256)}, u32[]{:S(2)}) copy-start(s32[192]{0:T(256)} %param.21) | copy-start | bytes 2308
  7.2 17.1 %copy-start.1 = (bf16[128,1,128]{2,0,1:T(8,128)(2,1)S(1)}, bf16[128,1,128]{2,0,1:T(8,128)(2,1)}, u32[]{:S(2)}) copy-start(bf16[128,1,128]{2,0,1:T(8,128)(2,1)} %param.18) | copy-start | bytes 98308
  7.2 18.0 %copy-start.3 = (bf16[128,1,16,64]{0,3,2,1:T(8,128)(2,1)S(1)}, bf16[128,1,16,64]{0,3,2,1:T(8,128)(2,1)}, u32[]{:S(2)}) copy-start(bf16[128,1,16,64]{0,3,2,1:T(8,128)(2,1)} %param.15) | copy-start | bytes 786436
  8.9 44.3 %all-to-all-start = ((bf16[16,16,1024]{2,1,0:T(8,128)(2,1)}), bf16[16,16,1024]{2,1,0:T(8,128)(2,1)S(1)}, u32[]{:S(2)}, u32[]{:S(2)}) async-start(bf16[16,16,1024]{2,1,0:T(8,128)(2,1)} %broadcast_in_dim.14), calls=%async_computation | async-start | bytes 1048576 | tf_op jit(solution)/shard_map/all_to_all | solution.py:35
  26.9 36.9 %copy-start.17 = (s32[192]{0:T(256)S(1)}, s32[192]{0:T(256)}, u32[]{:S(2)}) copy-start(s32[192]{0:T(256)} %param.22) | copy-start | bytes 2308
  27.0 37.0 %copy-start.11 = (bf16[384,128]{1,0:T(8,128)(2,1)S(1)}, bf16[384,128]{1,0:T(8,128)(2,1)}, u32[]{:S(2)}) copy-start(bf16[384,128]{1,0:T(8,128)(2,1)} %param.13) | copy-start | bytes 294916
  53.2 9.9 %copy-start.2 = (bf16[16,16,1024]{2,1,0:T(8,128)(2,1)}, bf16[16,16,1024]{2,1,0:T(8,128)(2,1)S(1)}, u32[]{:S(2)}) copy-start(bf16[16,16,1024]{2,1,0:T(8,128)(2,1)S(1)} %all-to-all-done) | copy-start | bytes 1572868
  53.2 44.5 %all-to-all-start.1 = ((bf16[64,3,1152]{2,1,0:T(4,128)(2,1)}), bf16[64,3,1152]{2,1,0:T(4,128)(2,1)S(1)}, u32[]{:S(2)}, u32[]{:S(2)}) async-start(bf16[64,3,1152]{2,1,0:T(4,128)(2,1)} %pad_maximum_fusion.1), calls=%async_computation.2 | async-start | bytes 1179648 | tf_op jit(solution)/shard_map/all_to_all | solution.py:86
  63.0 76.3 %all-gather.2.cloned.1.call-start = ((), (), s32[]{:S(2)}) async-start(), calls=%async_computation.4 | async-start | bytes 2621440 | tf_op jit(solution)/shard_map/all_gather | solution.py:37
  99.0 23.6 %copy-start.6 = (bf16[64,3,128]{2,1,0:T(4,128)(2,1)}, bf16[64,3,128]{2,1,0:T(4,128)(2,1)S(1)}, u32[]{:S(2)}) copy-start(bf16[64,3,128]{2,1,0:T(4,128)(2,1)S(1)} %slice.21) | copy-start | bytes 147460
  131.1 68.4 %all-to-all-start.2 = ((f32[3,64,1152]{2,0,1:T(4,128)}), f32[3,64,1152]{2,0,1:T(4,128)S(1)}, u32[]{:S(2)}, u32[]{:S(2)}) async-start(f32[3,64,1152]{2,0,1:T(4,128)} %copy.74), calls=%async_computation.3 | async-start | bytes 2359296 | tf_op jit(solution)/shard_map/all_to_all | solution.py:138
  139.3 66.5 %reduce-scatter.2.cloned.1.call-start = ((), (), s32[]{:S(2)}) async-start(), calls=%async_computation.5 | async-start | bytes 1769472 | tf_op jit(solution)/shard_map/reduce_scatter | solution.py:102
  143.1 14.4 %copy-start.7 = (bf16[64,3,128]{2,1,0:T(4,128)(2,1)S(1)}, bf16[64,3,128]{2,1,0:T(4,128)(2,1)}, u32[]{:S(2)}) copy-start(bf16[64,3,128]{2,1,0:T(4,128)(2,1)} %copy-done.6) | copy-start | bytes 147460
  143.1 14.4 %copy-start.10 = (bf16[3,128,64]{1,2,0:T(8,128)(2,1)S(1)}, bf16[3,128,64]{1,2,0:T(8,128)(2,1)}, u32[]{:S(2)}) copy-start(bf16[3,128,64]{1,2,0:T(8,128)(2,1)} %get-tuple-element.48) | copy-start | bytes 147460
  143.1 14.6 %copy-start.9 = (bf16[3,128,64]{1,2,0:T(8,128)(2,1)S(1)}, bf16[3,128,64]{1,2,0:T(8,128)(2,1)}, u32[]{:S(2)}) copy-start(bf16[3,128,64]{1,2,0:T(8,128)(2,1)} %copy-done.8) | copy-start | bytes 147460
  143.1 15.0 %copy-start.14 = (bf16[1024,1024]{0,1:T(8,128)(2,1)S(1)}, bf16[1024,1024]{0,1:T(8,128)(2,1)}, u32[]{:S(2)}) copy-start(bf16[1024,1024]{0,1:T(8,128)(2,1)} %all-gather.2.cloned.1.call-done) | copy-start | bytes 6291460
  199.5 2.1 copy-start.15
  199.5 2.1 copy-start.16
  201.5 0.9 slice-start.1
  201.5 1.8 slice-start
  201.5 2.8 %copy-start.4 = (f32[128,1,16,64]{0,3,2,1:T(8,128)S(1)}, f32[128,1,16,64]{0,3,2,1:T(8,128)}, u32[]{:S(2)}) copy-start(f32[128,1,16,64]{0,3,2,1:T(8,128)} %param.16) | copy-start | bytes 1572868
  201.5 2.8 %copy-start.5 = (f32[128,1,16,64]{0,3,2,1:T(8,128)S(1)}, f32[128,1,16,64]{0,3,2,1:T(8,128)}, u32[]{:S(2)}) copy-start(f32[128,1,16,64]{0,3,2,1:T(8,128)} %param.17) | copy-start | bytes 1572868
  (1 other events, 0.6 us)
Sparse Core Ops, SparseCore 0:
  66.5 40.3 all-gather.1
  143.3 39.2 reduce-scatter.1

commit v3 on v1

--- a/solution.py
+++ b/solution.py
@@ -28,9 +28,18 @@
 ADAPTER = ("ay", "az")
 
 
+def gather_along(piece, axis):
+    count = lax.axis_size(axis)
+    got = [piece]
+    for shift in range(1, count):
+        pairs = [(j, (j - shift) % count) for j in range(count)]
+        got.append(lax.ppermute(piece, axis, pairs))
+    ordered = jnp.roll(jnp.stack(got), lax.axis_index(axis), axis=0)
+    return jnp.moveaxis(ordered, 0, 1).reshape(piece.shape[0], count * piece.shape[1])
+
+
 def gather_weight(value_weight):
-    first = lax.all_gather(value_weight, "az", axis=1, tiled=True)
-    return lax.all_gather(first, "ay", axis=1, tiled=True)
+    return gather_along(gather_along(value_weight, "az"), "ay")
 
 
 def split_adapter(mesh):

time: 209 us -> 263 us (1.26)
  starting transfers between devices: 32.5 us -> 120 us
  blocking collectives: 93 us -> 38 us
  waiting for transfers between devices: 39.5 us -> 54 us
  local copies, waits for them, and re-layouts: 12.6 us -> 16.4 us
    ppermute x0 -> x18, starting transfers between devices: none -> 93.5 us  [gather_along(): got.append(lax.ppermute(piece, axis, pairs))]
    all_gather x1 -> x0, blocking collectives: 55.8 us -> none  [gather_weight(): first = lax.all_gather(value_weight, 'az', axis=1, tiled=True)]
    all_to_all x1, waiting for transfers between devices: 39.4 us -> 14.7 us  [shards(): lax.all_to_all(grads, ADAPTER, split_axis=1, concat_axis=0, tiled=True)]
    reduce_scatter x1, waiting for transfers between devices: 0.01 us -> 19.9 us  [shards(): lax.psum_scatter(frozen_part, 'mp', scatter_dimension=1, tiled=True)]
    ppermute x0 -> x18, waiting for transfers between devices: none -> 19.3 us  [gather_along(): got.append(lax.ppermute(piece, axis, pairs))]
    all_to_all x1, starting transfers between devices: 13.6 us -> 10.2 us  [shards(): lax.all_to_all(grads, ADAPTER, split_axis=1, concat_axis=0, tiled=True)]
    all_to_all x1, starting transfers between devices: 18.7 us -> 15.8 us  [shards(): lax.all_to_all(sent, ADAPTER, split_axis=0, concat_axis=0, tiled=True)]
  transfers between devices with their start and end apart: 4 -> 21, of which waited for: 1 -> 7; matrix products, arithmetic and copies ran while one was open for 9% -> 7% of each run, Pallas kernels for 0% -> 0%
where the time goes in v3:
time: 263 us; the launch traced here: 262 us
  starting transfers between devices  120 us (46%)
  waiting for transfers between devices  54 us (21%)
  blocking collectives  38 us (14%)
  local copies, waits for them, and re-layouts  16.4 us (6%)
  between operations  14.8 us (6%)
  matrix products  12.2 us (5%)
  other arithmetic  6.9 us (3%)
    ppermute x18, starting transfers between devices, gather_along(): got.append(lax.ppermute(piece, axis, pairs))  93.5 us
    psum x1, blocking collectives, shards(): down_sum = lax.psum(down_part, 'mp')  22.7 us
    reduce_scatter x1, waiting for transfers between devices, shards(): lax.psum_scatter(frozen_part, 'mp', scatter_dimension=1, tiled=True)  19.9 us
    ppermute x18, waiting for transfers between devices, gather_along(): got.append(lax.ppermute(piece, axis, pairs))  19.3 us
    all_to_all x1, starting transfers between devices, shards(): lax.all_to_all(sent, ADAPTER, split_axis=0, concat_axis=0, tiled=True)  15.8 us
    all_gather x1, blocking collectives, shards(): masked_full = lax.all_gather(masked_own, 'mp', axis=1, tiled=True)  15.3 us
    all_to_all x1, waiting for transfers between devices, shards(): lax.all_to_all(grads, ADAPTER, split_axis=1, concat_axis=0, tiled=True)  14.7 us
    all_to_all x1, starting transfers between devices, shards(): lax.all_to_all(grads, ADAPTER, split_axis=1, concat_axis=0, tiled=True)  10.2 us
  transfers between devices with their start and end apart: 21, of which 7 were waited for; matrix products, arithmetic and copies ran while one was open for 7% of the time, Pallas kernels for 0%

profile of v3, /device:TPU:6, one launch (start us, length us, event | category | flops | bytes accessed | tf_op | source)
XLA Modules:
  0.0 261.7 jit_solution(3475305058610863027)
XLA Ops:
  7.2 11.5 %collective-permute-start = (bf16[1024,16]{0,1:T(8,128)(2,1)}, bf16[1024,16]{0,1:T(8,128)(2,1)S(1)}, u32[]{:S(2)}, u32[]{:S(2)}) collective-permute-start(bf16[1024,16]{0,1:T(8,128)(2,1)} %param.14), channel_id=1, source_target_pairs={{0,120},{8,0},{16,8},{24,16},{32,24},{40,32},{48,40},{56,48},{64,5... | collective-permute-start | bytes 98312 | tf_op jit(solution)/shard_map/ppermute | solution.py:36
  18.7 3.4 %collective-permute-start.1 = (bf16[1024,16]{0,1:T(8,128)(2,1)}, bf16[1024,16]{0,1:T(8,128)(2,1)S(1)}, u32[]{:S(2)}, u32[]{:S(2)}) collective-permute-start(bf16[1024,16]{0,1:T(8,128)(2,1)} %param.14), channel_id=1, source_target_pairs={{0,112},{8,120},{16,0},{24,8},{32,16},{40,24},{48,32},{56,40},{64,... | collective-permute-start | bytes 98312 | tf_op jit(solution)/shard_map/ppermute | solution.py:36
  22.1 5.0 %collective-permute-start.2 = (bf16[1024,16]{0,1:T(8,128)(2,1)}, bf16[1024,16]{0,1:T(8,128)(2,1)S(1)}, u32[]{:S(2)}, u32[]{:S(2)}) collective-permute-start(bf16[1024,16]{0,1:T(8,128)(2,1)} %param.14), channel_id=1, source_target_pairs={{0,104},{8,112},{16,120},{24,0},{32,8},{40,16},{48,24},{56,32},{64... | collective-permute-start | bytes 98312 | tf_op jit(solution)/shard_map/ppermute | solution.py:36
  27.1 2.8 %collective-permute-start.3 = (bf16[1024,16]{0,1:T(8,128)(2,1)}, bf16[1024,16]{0,1:T(8,128)(2,1)S(1)}, u32[]{:S(2)}, u32[]{:S(2)}) collective-permute-start(bf16[1024,16]{0,1:T(8,128)(2,1)} %param.14), channel_id=1, source_target_pairs={{0,96},{8,104},{16,112},{24,120},{32,0},{40,8},{48,16},{56,24},{64... | collective-permute-start | bytes 98312 | tf_op jit(solution)/shard_map/ppermute | solution.py:36
  38.1 15.8 %all-to-all-start = ((bf16[64,3,1152]{2,1,0:T(4,128)(2,1)}), bf16[64,3,1152]{2,1,0:T(4,128)(2,1)S(1)}, u32[]{:S(2)}, u32[]{:S(2)}) async-start(bf16[64,3,1152]{2,1,0:T(4,128)(2,1)} %pad_maximum_fusion.1), calls=%async_computation.1 | async-start | bytes 1179648 | tf_op jit(solution)/shard_map/all_to_all | solution.py:91
  54.0 10.4 %collective-permute-start.5 = (bf16[1024,16]{0,1:T(8,128)(2,1)S(1)}, bf16[1024,16]{0,1:T(8,128)(2,1)S(1)}, u32[]{:S(2)}, u32[]{:S(2)}) collective-permute-start(bf16[1024,16]{0,1:T(8,128)(2,1)S(1)} %copy-done.3), channel_id=1, source_target_pairs={{0,80},{8,88},{16,96},{24,104},{32,112},{40,120},{48,0},{56,8},{64... | collective-permute-start | bytes 98312 | tf_op jit(solution)/shard_map/ppermute | solution.py:36
  64.4 4.3 %collective-permute-start.6 = (bf16[1024,16]{0,1:T(8,128)(2,1)S(1)}, bf16[1024,16]{0,1:T(8,128)(2,1)S(1)}, u32[]{:S(2)}, u32[]{:S(2)}) collective-permute-start(bf16[1024,16]{0,1:T(8,128)(2,1)S(1)} %copy-done.3), channel_id=1, source_target_pairs={{0,72},{8,80},{16,88},{24,96},{32,104},{40,112},{48,120},{56,0},{6... | collective-permute-start | bytes 98312 | tf_op jit(solution)/shard_map/ppermute | solution.py:36
  68.7 9.4 %collective-permute-start.7 = (bf16[1024,16]{0,1:T(8,128)(2,1)S(1)}, bf16[1024,16]{0,1:T(8,128)(2,1)S(1)}, u32[]{:S(2)}, u32[]{:S(2)}) collective-permute-start(bf16[1024,16]{0,1:T(8,128)(2,1)S(1)} %copy-done.3), channel_id=1, source_target_pairs={{0,64},{8,72},{16,80},{24,88},{32,96},{40,104},{48,112},{56,120},{... | collective-permute-start | bytes 98312 | tf_op jit(solution)/shard_map/ppermute | solution.py:36
  78.1 3.1 %collective-permute-start.8 = (bf16[1024,16]{0,1:T(8,128)(2,1)S(1)}, bf16[1024,16]{0,1:T(8,128)(2,1)S(1)}, u32[]{:S(2)}, u32[]{:S(2)}) collective-permute-start(bf16[1024,16]{0,1:T(8,128)(2,1)S(1)} %copy-done.3), channel_id=1, source_target_pairs={{0,56},{8,64},{16,72},{24,80},{32,88},{40,96},{48,104},{56,112},{6... | collective-permute-start | bytes 98312 | tf_op jit(solution)/shard_map/ppermute | solution.py:36
  81.2 10.3 %collective-permute-start.9 = (bf16[1024,16]{0,1:T(8,128)(2,1)S(1)}, bf16[1024,16]{0,1:T(8,128)(2,1)S(1)}, u32[]{:S(2)}, u32[]{:S(2)}) collective-permute-start(bf16[1024,16]{0,1:T(8,128)(2,1)S(1)} %copy-done.3), channel_id=1, source_target_pairs={{0,48},{8,56},{16,64},{24,72},{32,80},{40,88},{48,96},{56,104},{64... | collective-permute-start | bytes 98312 | tf_op jit(solution)/shard_map/ppermute | solution.py:36
  91.5 6.7 %collective-permute-start.10 = (bf16[1024,16]{0,1:T(8,128)(2,1)S(1)}, bf16[1024,16]{0,1:T(8,128)(2,1)S(1)}, u32[]{:S(2)}, u32[]{:S(2)}) collective-permute-start(bf16[1024,16]{0,1:T(8,128)(2,1)S(1)} %copy-done.3), channel_id=1, source_target_pairs={{0,40},{8,48},{16,56},{24,64},{32,72},{40,80},{48,88},{56,96},{64,... | collective-permute-start | bytes 98312 | tf_op jit(solution)/shard_map/ppermute | solution.py:36
  100.2 5.2 %collective-permute-start.12 = (bf16[1024,16]{0,1:T(8,128)(2,1)S(1)}, bf16[1024,16]{0,1:T(8,128)(2,1)S(1)}, u32[]{:S(2)}, u32[]{:S(2)}) collective-permute-start(bf16[1024,16]{0,1:T(8,128)(2,1)S(1)} %copy-done.3), channel_id=1, source_target_pairs={{0,24},{8,32},{16,40},{24,48},{32,56},{40,64},{48,72},{56,80},{64,... | collective-permute-start | bytes 98312 | tf_op jit(solution)/shard_map/ppermute | solution.py:36
  108.2 4.8 %collective-permute-start.14 = (bf16[1024,16]{0,1:T(8,128)(2,1)S(1)}, bf16[1024,16]{0,1:T(8,128)(2,1)S(1)}, u32[]{:S(2)}, u32[]{:S(2)}) collective-permute-start(bf16[1024,16]{0,1:T(8,128)(2,1)S(1)} %copy-done.3), channel_id=1, source_target_pairs={{0,8},{8,16},{16,24},{24,32},{32,40},{40,48},{48,56},{56,64},{64,7... | collective-permute-start | bytes 98312 | tf_op jit(solution)/shard_map/ppermute | solution.py:36
  115.4 4.8 %collective-permute-start.15 = (bf16[1024,256]{0,1:T(8,128)(2,1)S(1)}, bf16[1024,256]{0,1:T(8,128)(2,1)S(1)}, u32[]{:S(2)}, u32[]{:S(2)}) collective-permute-start(bf16[1024,256]{0,1:T(8,128)(2,1)S(1)} %bitcast.143), channel_id=1, source_target_pairs={{0,384},{128,0},{256,128},{384,256},{1,385},{129,1},{257,129},{385... | collective-permute-start | bytes 1572872 | tf_op jit(solution)/shard_map/ppermute | solution.py:36
  123.0 2.9 %collective-permute-start.17 = (bf16[1024,256]{0,1:T(8,128)(2,1)S(1)}, bf16[1024,256]{0,1:T(8,128)(2,1)S(1)}, u32[]{:S(2)}, u32[]{:S(2)}) collective-permute-start(bf16[1024,256]{0,1:T(8,128)(2,1)S(1)} %bitcast.145), channel_id=1, source_target_pairs={{0,128},{128,256},{256,384},{384,0},{1,129},{129,257},{257,385},{3... | collective-permute-start | bytes 1572872 | tf_op jit(solution)/shard_map/ppermute | solution.py:36
  125.9 11.5 %collective-permute-done.15 = bf16[1024,256]{0,1:T(8,128)(2,1)S(1)} collective-permute-done((bf16[1024,256]{0,1:T(8,128)(2,1)S(1)}, bf16[1024,256]{0,1:T(8,128)(2,1)S(1)}, u32[]{:S(2)}, u32[]{:S(2)}) %collective-permute-start.15) | collective-permute-done | bytes 524320 | tf_op jit(solution)/shard_map/ppermute | solution.py:36
  137.6 5.5 %collective-permute-done.17 = bf16[1024,256]{0,1:T(8,128)(2,1)S(1)} collective-permute-done((bf16[1024,256]{0,1:T(8,128)(2,1)S(1)}, bf16[1024,256]{0,1:T(8,128)(2,1)S(1)}, u32[]{:S(2)}, u32[]{:S(2)}) %collective-permute-start.17) | collective-permute-done | bytes 524320 | tf_op jit(solution)/shard_map/ppermute | solution.py:36
  146.4 22.7 %all-reduce.2 = (bf16[3,128,64]{1,2,0:T(8,128)(2,1)S(1)}, bf16[3,128,64]{1,2,0:T(8,128)(2,1)S(1)}) all-reduce(f32[3,128,64]{1,2,0:T(8,128)S(1)} %convolution_bitcast_fusion.2, f32[3,128,64]{1,2,0:T(8,128)S(1)} %convolution_multiply_fusion.2), channel_id=1, replica_groups=mesh['ay'=4,'az'=16,'mp'=8] {'mp'}, use_global_device_ids=true, to_apply=%region_2.3 | all-reduce | flops 49152 | bytes 294912 | tf_op jit(solution)/shard_map/psum | solution.py:111
  176.1 10.2 %all-to-all-start.1 = ((f32[3,64,1152]{2,0,1:T(4,128)}), f32[3,64,1152]{2,0,1:T(4,128)S(1)}, u32[]{:S(2)}, u32[]{:S(2)}) async-start(f32[3,64,1152]{2,0,1:T(4,128)} %copy.83), calls=%async_computation.2 | async-start | bytes 2359296 | tf_op jit(solution)/shard_map/all_to_all | solution.py:143
  186.4 4.0 %convolution_bitcast_fusion = f32[384,1024]{0,1:T(8,128)} fusion(bf16[1024,1024]{0,1:T(8,128)(2,1)} %bitcast.150, bf16[384,1024]{1,0:T(8,128)(2,1)S(1)} %copy-done), kind=kOutput, calls=%fused_computation.4 | convolution fusion | flops 805306368 | bytes 4456448 | tf_op jit(solution)/shard_map/dot_general | solution.py:102
  190.4 15.3 %all_gather.3 = bf16[384,1024]{1,0:T(8,128)(2,1)} all-gather(bf16[384,128]{1,0:T(8,128)(2,1)S(1)} %broadcast_multiply_fusion), channel_id=1, replica_groups=mesh['ay'=4,'az'=16,'mp'=8] {'mp'}, dimensions={1}, use_global_device_ids=true | all-gather | bytes 884736 | tf_op jit(solution)/shard_map/all_gather | solution.py:84
  206.5 3.7 %fusion = bf16[384,1024]{1,0:T(8,128)(2,1)} fusion(f32[3,128,1024]{2,1,0:T(8,128)S(1)} %fusion.19, bf16[384,1024]{1,0:T(8,128)(2,1)} %all_gather.3, bf16[1024,1024]{0,1:T(8,128)(2,1)} %bitcast.151), kind=kOutput, calls=%fused_computation.3 | convolution fusion | flops 806092800 | bytes 5242880 | tf_op jit(solution)/shard_map/dot_general | solution.py:124
  210.2 19.9 %reduce-scatter.2.cloned.1.call-done = f32[384,128]{0,1:T(8,128)} async-done(((f32[384,1024]{0,1:T(8,128)}), f32[384,128]{0,1:T(8,128)}) %reduce-scatter.2.cloned.1.call-update) | async-done | bytes 196624 | tf_op jit(solution)/shard_map/reduce_scatter | solution.py:107
  231.8 14.7 %all-to-all-done.1 = f32[3,64,1152]{2,0,1:T(4,128)S(1)} async-done(((f32[3,64,1152]{2,0,1:T(4,128)}), f32[3,64,1152]{2,0,1:T(4,128)S(1)}, u32[]{:S(2)}, u32[]{:S(2)}) %all-to-all-start.1) | async-done | bytes 884768 | tf_op jit(solution)/shard_map/all_to_all | solution.py:143
  (117 shorter events, 39.1 us)
Async XLA Ops:
  7.2 138.8 %copy-start = (bf16[384,1024]{1,0:T(8,128)(2,1)S(1)}, bf16[384,1024]{1,0:T(8,128)(2,1)}, u32[]{:S(2)}) copy-start(bf16[384,1024]{1,0:T(8,128)(2,1)} %param.12) | copy-start | bytes 2359300
  7.2 46.7 %copy-start.7 = (s32[192]{0:T(256)S(1)}, s32[192]{0:T(256)}, u32[]{:S(2)}) copy-start(s32[192]{0:T(256)} %param.22) | copy-start | bytes 2308
  7.2 46.8 %collective-permute-start = (bf16[1024,16]{0,1:T(8,128)(2,1)}, bf16[1024,16]{0,1:T(8,128)(2,1)S(1)}, u32[]{:S(2)}, u32[]{:S(2)}) collective-permute-start(bf16[1024,16]{0,1:T(8,128)(2,1)} %param.14), channel_id=1, source_target_pairs={{0,120},{8,0},{16,8},{24,16},{32,24},{40,32},{48,40},{56,48},{64,5... | collective-permute-start | bytes 98312 | tf_op jit(solution)/shard_map/ppermute | solution.py:36
  18.7 45.7 %collective-permute-start.1 = (bf16[1024,16]{0,1:T(8,128)(2,1)}, bf16[1024,16]{0,1:T(8,128)(2,1)S(1)}, u32[]{:S(2)}, u32[]{:S(2)}) collective-permute-start(bf16[1024,16]{0,1:T(8,128)(2,1)} %param.14), channel_id=1, source_target_pairs={{0,112},{8,120},{16,0},{24,8},{32,16},{40,24},{48,32},{56,40},{64,... | collective-permute-start | bytes 98312 | tf_op jit(solution)/shard_map/ppermute | solution.py:36
  22.1 46.6 %collective-permute-start.2 = (bf16[1024,16]{0,1:T(8,128)(2,1)}, bf16[1024,16]{0,1:T(8,128)(2,1)S(1)}, u32[]{:S(2)}, u32[]{:S(2)}) collective-permute-start(bf16[1024,16]{0,1:T(8,128)(2,1)} %param.14), channel_id=1, source_target_pairs={{0,104},{8,112},{16,120},{24,0},{32,8},{40,16},{48,24},{56,32},{64... | collective-permute-start | bytes 98312 | tf_op jit(solution)/shard_map/ppermute | solution.py:36
  27.1 51.0 %collective-permute-start.3 = (bf16[1024,16]{0,1:T(8,128)(2,1)}, bf16[1024,16]{0,1:T(8,128)(2,1)S(1)}, u32[]{:S(2)}, u32[]{:S(2)}) collective-permute-start(bf16[1024,16]{0,1:T(8,128)(2,1)} %param.14), channel_id=1, source_target_pairs={{0,96},{8,104},{16,112},{24,120},{32,0},{40,8},{48,16},{56,24},{64... | collective-permute-start | bytes 98312 | tf_op jit(solution)/shard_map/ppermute | solution.py:36
  30.0 51.3 %collective-permute-start.4 = (bf16[1024,16]{0,1:T(8,128)(2,1)}, bf16[1024,16]{0,1:T(8,128)(2,1)S(1)}, u32[]{:S(2)}, u32[]{:S(2)}) collective-permute-start(bf16[1024,16]{0,1:T(8,128)(2,1)} %param.14), channel_id=1, source_target_pairs={{0,88},{8,96},{16,104},{24,112},{32,120},{40,0},{48,8},{56,16},{64... | collective-permute-start | bytes 98312 | tf_op jit(solution)/shard_map/ppermute | solution.py:36
  34.2 88.7 %copy-start.4 = (bf16[384,128]{1,0:T(8,128)(2,1)S(1)}, bf16[384,128]{1,0:T(8,128)(2,1)}, u32[]{:S(2)}) copy-start(bf16[384,128]{1,0:T(8,128)(2,1)} %param.13) | copy-start | bytes 294916
  38.1 106.8 %all-to-all-start = ((bf16[64,3,1152]{2,1,0:T(4,128)(2,1)}), bf16[64,3,1152]{2,1,0:T(4,128)(2,1)S(1)}, u32[]{:S(2)}, u32[]{:S(2)}) async-start(bf16[64,3,1152]{2,1,0:T(4,128)(2,1)} %pad_maximum_fusion.1), calls=%async_computation.1 | async-start | bytes 1179648 | tf_op jit(solution)/shard_map/all_to_all | solution.py:91
  54.0 37.5 %collective-permute-start.5 = (bf16[1024,16]{0,1:T(8,128)(2,1)S(1)}, bf16[1024,16]{0,1:T(8,128)(2,1)S(1)}, u32[]{:S(2)}, u32[]{:S(2)}) collective-permute-start(bf16[1024,16]{0,1:T(8,128)(2,1)S(1)} %copy-done.3), channel_id=1, source_target_pairs={{0,80},{8,88},{16,96},{24,104},{32,112},{40,120},{48,0},{56,8},{64... | collective-permute-start | bytes 98312 | tf_op jit(solution)/shard_map/ppermute | solution.py:36
  64.4 33.8 %collective-permute-start.6 = (bf16[1024,16]{0,1:T(8,128)(2,1)S(1)}, bf16[1024,16]{0,1:T(8,128)(2,1)S(1)}, u32[]{:S(2)}, u32[]{:S(2)}) collective-permute-start(bf16[1024,16]{0,1:T(8,128)(2,1)S(1)} %copy-done.3), channel_id=1, source_target_pairs={{0,72},{8,80},{16,88},{24,96},{32,104},{40,112},{48,120},{56,0},{6... | collective-permute-start | bytes 98312 | tf_op jit(solution)/shard_map/ppermute | solution.py:36
  68.7 31.5 %collective-permute-start.7 = (bf16[1024,16]{0,1:T(8,128)(2,1)S(1)}, bf16[1024,16]{0,1:T(8,128)(2,1)S(1)}, u32[]{:S(2)}, u32[]{:S(2)}) collective-permute-start(bf16[1024,16]{0,1:T(8,128)(2,1)S(1)} %copy-done.3), channel_id=1, source_target_pairs={{0,64},{8,72},{16,80},{24,88},{32,96},{40,104},{48,112},{56,120},{... | collective-permute-start | bytes 98312 | tf_op jit(solution)/shard_map/ppermute | solution.py:36
  78.1 27.3 %collective-permute-start.8 = (bf16[1024,16]{0,1:T(8,128)(2,1)S(1)}, bf16[1024,16]{0,1:T(8,128)(2,1)S(1)}, u32[]{:S(2)}, u32[]{:S(2)}) collective-permute-start(bf16[1024,16]{0,1:T(8,128)(2,1)S(1)} %copy-done.3), channel_id=1, source_target_pairs={{0,56},{8,64},{16,72},{24,80},{32,88},{40,96},{48,104},{56,112},{6... | collective-permute-start | bytes 98312 | tf_op jit(solution)/shard_map/ppermute | solution.py:36
  81.2 26.9 %collective-permute-start.9 = (bf16[1024,16]{0,1:T(8,128)(2,1)S(1)}, bf16[1024,16]{0,1:T(8,128)(2,1)S(1)}, u32[]{:S(2)}, u32[]{:S(2)}) collective-permute-start(bf16[1024,16]{0,1:T(8,128)(2,1)S(1)} %copy-done.3), channel_id=1, source_target_pairs={{0,48},{8,56},{16,64},{24,72},{32,80},{40,88},{48,96},{56,104},{64... | collective-permute-start | bytes 98312 | tf_op jit(solution)/shard_map/ppermute | solution.py:36
  91.5 21.4 %collective-permute-start.10 = (bf16[1024,16]{0,1:T(8,128)(2,1)S(1)}, bf16[1024,16]{0,1:T(8,128)(2,1)S(1)}, u32[]{:S(2)}, u32[]{:S(2)}) collective-permute-start(bf16[1024,16]{0,1:T(8,128)(2,1)S(1)} %copy-done.3), channel_id=1, source_target_pairs={{0,40},{8,48},{16,56},{24,64},{32,72},{40,80},{48,88},{56,96},{64,... | collective-permute-start | bytes 98312 | tf_op jit(solution)/shard_map/ppermute | solution.py:36
  98.3 14.7 %collective-permute-start.11 = (bf16[1024,16]{0,1:T(8,128)(2,1)S(1)}, bf16[1024,16]{0,1:T(8,128)(2,1)S(1)}, u32[]{:S(2)}, u32[]{:S(2)}) collective-permute-start(bf16[1024,16]{0,1:T(8,128)(2,1)S(1)} %copy-done.3), channel_id=1, source_target_pairs={{0,32},{8,40},{16,48},{24,56},{32,64},{40,72},{48,80},{56,88},{64,... | collective-permute-start | bytes 98312 | tf_op jit(solution)/shard_map/ppermute | solution.py:36
  100.2 12.8 %collective-permute-start.12 = (bf16[1024,16]{0,1:T(8,128)(2,1)S(1)}, bf16[1024,16]{0,1:T(8,128)(2,1)S(1)}, u32[]{:S(2)}, u32[]{:S(2)}) collective-permute-start(bf16[1024,16]{0,1:T(8,128)(2,1)S(1)} %copy-done.3), channel_id=1, source_target_pairs={{0,24},{8,32},{16,40},{24,48},{32,56},{40,64},{48,72},{56,80},{64,... | collective-permute-start | bytes 98312 | tf_op jit(solution)/shard_map/ppermute | solution.py:36
  105.5 7.9 %collective-permute-start.13 = (bf16[1024,16]{0,1:T(8,128)(2,1)S(1)}, bf16[1024,16]{0,1:T(8,128)(2,1)S(1)}, u32[]{:S(2)}, u32[]{:S(2)}) collective-permute-start(bf16[1024,16]{0,1:T(8,128)(2,1)S(1)} %copy-done.3), channel_id=1, source_target_pairs={{0,16},{8,24},{16,32},{24,40},{32,48},{40,56},{48,64},{56,72},{64,... | collective-permute-start | bytes 98312 | tf_op jit(solution)/shard_map/ppermute | solution.py:36
  108.2 7.0 %collective-permute-start.14 = (bf16[1024,16]{0,1:T(8,128)(2,1)S(1)}, bf16[1024,16]{0,1:T(8,128)(2,1)S(1)}, u32[]{:S(2)}, u32[]{:S(2)}) collective-permute-start(bf16[1024,16]{0,1:T(8,128)(2,1)S(1)} %copy-done.3), channel_id=1, source_target_pairs={{0,8},{8,16},{16,24},{24,32},{32,40},{40,48},{48,56},{56,64},{64,7... | collective-permute-start | bytes 98312 | tf_op jit(solution)/shard_map/ppermute | solution.py:36
  115.4 22.0 %collective-permute-start.15 = (bf16[1024,256]{0,1:T(8,128)(2,1)S(1)}, bf16[1024,256]{0,1:T(8,128)(2,1)S(1)}, u32[]{:S(2)}, u32[]{:S(2)}) collective-permute-start(bf16[1024,256]{0,1:T(8,128)(2,1)S(1)} %bitcast.143), channel_id=1, source_target_pairs={{0,384},{128,0},{256,128},{384,256},{1,385},{129,1},{257,129},{385... | collective-permute-start | bytes 1572872 | tf_op jit(solution)/shard_map/ppermute | solution.py:36
  120.3 17.2 %collective-permute-start.16 = (bf16[1024,256]{0,1:T(8,128)(2,1)S(1)}, bf16[1024,256]{0,1:T(8,128)(2,1)S(1)}, u32[]{:S(2)}, u32[]{:S(2)}) collective-permute-start(bf16[1024,256]{0,1:T(8,128)(2,1)S(1)} %bitcast.144), channel_id=1, source_target_pairs={{0,256},{128,384},{256,0},{384,128},{1,257},{129,385},{257,1},{385... | collective-permute-start | bytes 1572872 | tf_op jit(solution)/shard_map/ppermute | solution.py:36
  123.0 20.1 %collective-permute-start.17 = (bf16[1024,256]{0,1:T(8,128)(2,1)S(1)}, bf16[1024,256]{0,1:T(8,128)(2,1)S(1)}, u32[]{:S(2)}, u32[]{:S(2)}) collective-permute-start(bf16[1024,256]{0,1:T(8,128)(2,1)S(1)} %bitcast.145), channel_id=1, source_target_pairs={{0,128},{128,256},{256,384},{384,0},{1,129},{129,257},{257,385},{3... | collective-permute-start | bytes 1572872 | tf_op jit(solution)/shard_map/ppermute | solution.py:36
  176.1 70.4 %all-to-all-start.1 = ((f32[3,64,1152]{2,0,1:T(4,128)}), f32[3,64,1152]{2,0,1:T(4,128)S(1)}, u32[]{:S(2)}, u32[]{:S(2)}) async-start(f32[3,64,1152]{2,0,1:T(4,128)} %copy.83), calls=%async_computation.2 | async-start | bytes 2359296 | tf_op jit(solution)/shard_map/all_to_all | solution.py:143
  186.4 43.7 %reduce-scatter.2.cloned.1.call-start = ((), (), s32[]{:S(2)}) async-start(), calls=%async_computation.3 | async-start | bytes 1769472 | tf_op jit(solution)/shard_map/reduce_scatter | solution.py:107
  (6 other events, 115.3 us)
Sparse Core Ops, SparseCore 0:
  190.5 39.4 reduce-scatter.1

commit v4 on v1

--- a/solution.py
+++ b/solution.py
@@ -29,8 +29,13 @@
 
 
 def gather_weight(value_weight):
-    first = lax.all_gather(value_weight, "az", axis=1, tiled=True)
-    return lax.all_gather(first, "ay", axis=1, tiled=True)
+    rows, cols = value_weight.shape
+    n_y = lax.axis_size("ay")
+    n_z = lax.axis_size("az")
+    first = lax.all_gather(value_weight, "ay", axis=1, tiled=True)
+    whole = lax.all_gather(first, "az", axis=1, tiled=True)
+    whole = whole.reshape(rows, n_z, n_y, cols).transpose(0, 2, 1, 3)
+    return whole.reshape(rows, n_y * n_z * cols)
 
 
 def split_adapter(mesh):

time: 209 us -> 198 us (0.947)
  blocking collectives: 93 us -> 51.7 us
  waiting for transfers between devices: 39.5 us -> 77.3 us
  starting transfers between devices: 32.5 us -> 23.8 us
  local copies, waits for them, and re-layouts: 12.6 us -> 15.7 us
    all_gather x1, blocking collectives: 55.8 us -> 14.2 us  [gather_weight(): first = lax.all_gather(value_weight, 'ay', axis=1, tiled=True)]
    all_to_all x1, waiting for transfers between devices: 0.01 us -> 39.2 us  [shards(): lax.all_to_all(sent, ADAPTER, split_axis=0, concat_axis=0, tiled=True)]
    all_to_all x1, starting transfers between devices: 13.6 us -> 6.32 us  [shards(): lax.all_to_all(grads, ADAPTER, split_axis=1, concat_axis=0, tiled=True)]
  transfers between devices with their start and end apart: 4 -> 4, of which waited for: 1 -> 2; matrix products, arithmetic and copies ran while one was open for 9% -> 12% of each run, Pallas kernels for 0% -> 0%
where the time goes in v4:
time: 198 us
  waiting for transfers between devices  77.3 us (39%)
  blocking collectives  51.7 us (26%)
  starting transfers between devices  23.8 us (12%)
  local copies, waits for them, and re-layouts  15.7 us (8%)
  between operations  14.3 us (7%)
  matrix products  8.49 us (4%)
  other arithmetic  6.45 us (3%)
    all_to_all x1, waiting for transfers between devices, shards(): lax.all_to_all(sent, ADAPTER, split_axis=0, concat_axis=0, tiled=True)  39.2 us
    all_to_all x1, waiting for transfers between devices, shards(): lax.all_to_all(grads, ADAPTER, split_axis=1, concat_axis=0, tiled=True)  38 us
    psum x1, blocking collectives, shards(): down_sum = lax.psum(down_part, 'mp')  23.2 us
    all_to_all x1, starting transfers between devices, shards(): lax.all_to_all(sent, ADAPTER, split_axis=0, concat_axis=0, tiled=True)  17.4 us
    all_gather x1, blocking collectives, shards(): masked_full = lax.all_gather(masked_own, 'mp', axis=1, tiled=True)  14.3 us
    all_gather x1, blocking collectives, gather_weight(): first = lax.all_gather(value_weight, 'ay', axis=1, tiled=True)  14.2 us
    all_to_all x1, starting transfers between devices, shards(): lax.all_to_all(grads, ADAPTER, split_axis=1, concat_axis=0, tiled=True)  6.32 us
  transfers between devices with their start and end apart: 4, of which 2 were waited for; matrix products, arithmetic and copies ran while one was open for 12% of the time, Pallas kernels for 0%

profile of v4, /device:TPU:6, one launch (start us, length us, event | category | flops | bytes accessed | tf_op | source)
XLA Modules:
  0.0 197.8 jit_solution(9538932899444765746)
XLA Ops:
  7.2 14.2 %all_gather.9 = bf16[1024,64]{0,1:T(8,128)(2,1)} all-gather(bf16[1024,16]{0,1:T(8,128)(2,1)} %param.14), channel_id=1, replica_groups=mesh['ay'=4,'az'=16,'mp'=8] {'ay'}, dimensions={1}, use_global_device_ids=true | all-gather | bytes 163840 | tf_op jit(solution)/shard_map/all_gather | solution.py:35
  22.4 1.5 gather_fusion.1
  23.9 1.4 copy.85
  26.6 1.1 pad_maximum_fusion.1
  27.7 17.4 %all-to-all-start = ((bf16[64,3,1152]{2,1,0:T(4,128)(2,1)}), bf16[64,3,1152]{2,1,0:T(4,128)(2,1)S(1)}, u32[]{:S(2)}, u32[]{:S(2)}) async-start(bf16[64,3,1152]{2,1,0:T(4,128)(2,1)} %pad_maximum_fusion.1), calls=%async_computation.1 | async-start | bytes 1179648 | tf_op jit(solution)/shard_map/all_to_all | solution.py:87
  45.4 39.2 %all-to-all-done = bf16[64,3,1152]{2,1,0:T(4,128)(2,1)S(1)} async-done(((bf16[64,3,1152]{2,1,0:T(4,128)(2,1)}), bf16[64,3,1152]{2,1,0:T(4,128)(2,1)S(1)}, u32[]{:S(2)}, u32[]{:S(2)}) %all-to-all-start) | async-done | bytes 442400 | tf_op jit(solution)/shard_map/all_to_all | solution.py:87
  86.1 23.2 %all-reduce.2 = (bf16[3,128,64]{1,2,0:T(8,128)(2,1)S(1)}, bf16[3,128,64]{1,2,0:T(8,128)(2,1)S(1)}) all-reduce(f32[3,128,64]{1,2,0:T(8,128)S(1)} %convolution_bitcast_fusion.1, f32[3,128,64]{1,2,0:T(8,128)S(1)} %convolution_multiply_fusion.2), channel_id=1, replica_groups=mesh['ay'=4,'az'=16,'mp'=8] {'mp'}, use_global_device_ids=true, to_apply=%region_2.3 | all-reduce | flops 49152 | bytes 294912 | tf_op jit(solution)/shard_map/psum | solution.py:107
  109.3 1.1 convolution_bitcast_fusion
  110.4 1.6 copy.90
  112.0 1.3 reshape.151
  113.5 1.2 pad_maximum_fusion
  114.7 1.6 copy.91
  116.4 6.3 %all-to-all-start.1 = ((f32[3,64,1152]{2,0,1:T(4,128)}), f32[3,64,1152]{2,0,1:T(4,128)S(1)}, u32[]{:S(2)}, u32[]{:S(2)}) async-start(f32[3,64,1152]{2,0,1:T(4,128)} %copy.91), calls=%async_computation.2 | async-start | bytes 2359296 | tf_op jit(solution)/shard_map/all_to_all | solution.py:139
  122.8 1.8 copy.84
  124.6 1.3 copy-done.2
  125.9 2.2 %fusion.21 = f32[384,1024]{1,0:T(8,128)} fusion(bf16[384,1024]{1,0:T(8,128)(2,1)S(1)} %copy-done, bf16[1024,1024]{0,1:T(8,128)(2,1)S(1)} %bitcast.84), kind=kOutput, calls=%fused_computation.45 | convolution fusion | flops 805306368 | bytes 4456448 | tf_op jit(solution)/shard_map/dot_general | solution.py:98
  128.1 14.3 %all_gather.11 = bf16[384,1024]{1,0:T(8,128)(2,1)S(1)} all-gather(bf16[384,128]{1,0:T(8,128)(2,1)S(1)} %broadcast_multiply_fusion), channel_id=1, replica_groups=mesh['ay'=4,'az'=16,'mp'=8] {'mp'}, dimensions={1}, use_global_device_ids=true | all-gather | bytes 884736 | tf_op jit(solution)/shard_map/all_gather | solution.py:80
  143.1 1.9 fusion
  145.0 38.0 %all-to-all-done.1 = f32[3,64,1152]{2,0,1:T(4,128)S(1)} async-done(((f32[3,64,1152]{2,0,1:T(4,128)}), f32[3,64,1152]{2,0,1:T(4,128)S(1)}, u32[]{:S(2)}, u32[]{:S(2)}) %all-to-all-start.1) | async-done | bytes 884768 | tf_op jit(solution)/shard_map/all_to_all | solution.py:139
  183.0 2.0 %all_to_all.21 = f32[192,1,1152]{2,1,0:T(1,128)} reshape(f32[64,3,1,1152]{3,1,0,2:T(4,128)S(1)} %bitcast.80) | data formatting | bytes 1769472 | tf_op jit(solution)/shard_map/all_to_all | solution.py:139
  185.9 0.9 divide_subtract_fusion.1
  186.8 1.0 fusion.1
  187.9 1.4 divide_subtract_fusion
  189.3 1.7 fusion.6
  (49 shorter events, 5.8 us)
Async XLA Ops:
  7.2 78.3 %copy-start = (bf16[384,1024]{1,0:T(8,128)(2,1)S(1)}, bf16[384,1024]{1,0:T(8,128)(2,1)}, u32[]{:S(2)}) copy-start(bf16[384,1024]{1,0:T(8,128)(2,1)} %param.12) | copy-start | bytes 2359300
  7.2 115.6 %all-gather.2.cloned.1.call-start = ((), (), s32[]{:S(2)}) async-start(), calls=%async_computation.3 | async-start | bytes 2228224 | tf_op jit(solution)/shard_map/all_gather | solution.py:36
  26.1 19.1 %copy-start.10 = (s32[192]{0:T(256)S(1)}, s32[192]{0:T(256)}, u32[]{:S(2)}) copy-start(s32[192]{0:T(256)} %param.22) | copy-start | bytes 2308
  26.1 19.2 %copy-start.7 = (bf16[384,128]{1,0:T(8,128)(2,1)S(1)}, bf16[384,128]{1,0:T(8,128)(2,1)}, u32[]{:S(2)}) copy-start(bf16[384,128]{1,0:T(8,128)(2,1)} %param.13) | copy-start | bytes 294916
  27.7 56.9 %all-to-all-start = ((bf16[64,3,1152]{2,1,0:T(4,128)(2,1)}), bf16[64,3,1152]{2,1,0:T(4,128)(2,1)S(1)}, u32[]{:S(2)}, u32[]{:S(2)}) async-start(bf16[64,3,1152]{2,1,0:T(4,128)(2,1)} %pad_maximum_fusion.1), calls=%async_computation.1 | async-start | bytes 1179648 | tf_op jit(solution)/shard_map/all_to_all | solution.py:87
  116.4 66.6 %all-to-all-start.1 = ((f32[3,64,1152]{2,0,1:T(4,128)}), f32[3,64,1152]{2,0,1:T(4,128)S(1)}, u32[]{:S(2)}, u32[]{:S(2)}) async-start(f32[3,64,1152]{2,0,1:T(4,128)} %copy.91), calls=%async_computation.2 | async-start | bytes 2359296 | tf_op jit(solution)/shard_map/all_to_all | solution.py:139
  122.7 66.6 %reduce-scatter.2.cloned.1.call-start = ((), (), s32[]{:S(2)}) async-start(), calls=%async_computation.4 | async-start | bytes 1769472 | tf_op jit(solution)/shard_map/reduce_scatter | solution.py:103
  124.5 1.3 copy-start.2
  128.1 15.0 %copy-start.3 = (bf16[1024,4,16,16]{0,3,2,1:T(8,128)(2,1)S(1)}, bf16[1024,4,16,16]{0,3,2,1:T(8,128)(2,1)}, u32[]{:S(2)}) copy-start(bf16[1024,4,16,16]{0,3,2,1:T(8,128)(2,1)} %copy-done.2) | copy-start | bytes 6291460
  183.0 2.1 %copy-start.1 = (bf16[128,1,128]{2,0,1:T(8,128)(2,1)S(1)}, bf16[128,1,128]{2,0,1:T(8,128)(2,1)}, u32[]{:S(2)}) copy-start(bf16[128,1,128]{2,0,1:T(8,128)(2,1)} %param.18) | copy-start | bytes 98308
  183.0 2.1 %copy-start.8 = (f32[128,1,128]{2,1,0:T(1,128)S(1)}, f32[128,1,128]{2,1,0:T(1,128)}, u32[]{:S(2)}) copy-start(f32[128,1,128]{2,1,0:T(1,128)} %param.19) | copy-start | bytes 196612
  183.0 2.1 %copy-start.9 = (f32[128,1,128]{2,1,0:T(1,128)S(1)}, f32[128,1,128]{2,1,0:T(1,128)}, u32[]{:S(2)}) copy-start(f32[128,1,128]{2,1,0:T(1,128)} %param.20) | copy-start | bytes 196612
  185.0 0.9 slice-start.1
  185.0 1.8 slice-start
  185.0 2.8 %copy-start.4 = (bf16[128,1,16,64]{0,3,2,1:T(8,128)(2,1)S(1)}, bf16[128,1,16,64]{0,3,2,1:T(8,128)(2,1)}, u32[]{:S(2)}) copy-start(bf16[128,1,16,64]{0,3,2,1:T(8,128)(2,1)} %param.15) | copy-start | bytes 786436
  185.0 2.8 %copy-start.5 = (f32[128,1,16,64]{0,3,2,1:T(8,128)S(1)}, f32[128,1,16,64]{0,3,2,1:T(8,128)}, u32[]{:S(2)}) copy-start(f32[128,1,16,64]{0,3,2,1:T(8,128)} %param.16) | copy-start | bytes 1572868
  185.0 2.8 %copy-start.6 = (f32[128,1,16,64]{0,3,2,1:T(8,128)S(1)}, f32[128,1,16,64]{0,3,2,1:T(8,128)}, u32[]{:S(2)}) copy-start(f32[128,1,16,64]{0,3,2,1:T(8,128)} %param.17) | copy-start | bytes 1572868
Sparse Core Ops, SparseCore 0:
  21.6 91.0 all-gather.1
  128.2 39.4 reduce-scatter.1

commit v5 on v4

--- a/solution.py
+++ b/solution.py
@@ -36,6 +36,16 @@
     whole = lax.all_gather(first, "az", axis=1, tiled=True)
     whole = whole.reshape(rows, n_z, n_y, cols).transpose(0, 2, 1, 3)
     return whole.reshape(rows, n_y * n_z * cols)
+
+
+def exchange(x, axis):
+    n_y = lax.axis_size("ay")
+    n_z = lax.axis_size("az")
+    shape = x.shape
+    x = x.reshape(shape[:axis] + (n_y, n_z, shape[axis] // (n_y * n_z)) + shape[axis + 1 :])
+    x = lax.all_to_all(x, "az", split_axis=axis + 1, concat_axis=axis + 1, tiled=True)
+    x = lax.all_to_all(x, "ay", split_axis=axis, concat_axis=axis, tiled=True)
+    return x.reshape(shape)
 
 
 def split_adapter(mesh):
@@ -84,7 +94,7 @@
     sent_down = down_store[:, 0][tile_adapter_slot].reshape(tile_total, row_part * rank)
     sent_up = up_store[tile_adapter_slot].reshape(tile_total, head_cols)
     sent = jnp.concatenate([sent_down, sent_up], axis=1)
-    arrived = lax.all_to_all(sent, ADAPTER, split_axis=0, concat_axis=0, tiled=True)
+    arrived = exchange(sent, 0)
     arrived = arrived.reshape(n_adapter, tiles_here, row_part * rank + head_cols)
     down_panel = (
         arrived[:, :, : row_part * rank]
@@ -136,9 +146,9 @@
     grads = jnp.concatenate(
         [home_down.reshape(tiles_here, n_adapter, row_part * rank), local_up_weight], axis=2
     )
-    grads = lax.all_to_all(grads, ADAPTER, split_axis=1, concat_axis=0, tiled=True)
-    arrived_down = grads[:, 0, : row_part * rank]
-    arrived_up = grads[:, 0, row_part * rank :]
+    grads = exchange(grads, 1).transpose(1, 0, 2).reshape(tile_total, -1)
+    arrived_down = grads[:, : row_part * rank]
+    arrived_up = grads[:, row_part * rank :]
     selector = (adapter_ids[:, None] == tile_adapter_slot[None, :]).astype(jnp.float32)
     down_gradient = jnp.dot(
         selector, arrived_down.reshape(tile_total, -1), precision=lax.Precision.HIGHEST

time: 198 us -> 186 us (0.939)
  the two profiles are of different devices: /device:TPU:6 before, /device:TPU:32 now
where the time goes in v5:
time: 186 us; the launch traced here: 185 us
  blocking collectives  58 us (31%)
  waiting for transfers between devices  46.3 us (25%)
  starting transfers between devices  35.3 us (19%)
  local copies, waits for them, and re-layouts  16.3 us (9%)
  between operations  14.4 us (8%)
  matrix products  9.44 us (5%)
  other arithmetic  5.7 us (3%)
    all_to_all x2, starting transfers between devices, exchange(): lax.all_to_all(x, 'az', split_axis=axis + 1, concat_axis=axis + 1, tiled=...  25.7 us
    psum x1, blocking collectives, shards(): down_sum = lax.psum(down_part, 'mp')  25.5 us
    all_gather x1, blocking collectives, shards(): masked_full = lax.all_gather(masked_own, 'mp', axis=1, tiled=True)  19.3 us
    all_gather x1, waiting for transfers between devices, gather_weight(): whole = lax.all_gather(first, 'az', axis=1, tiled=True)  18.7 us
    all_to_all x2, waiting for transfers between devices, exchange(): x = lax.all_to_all(x, 'ay', split_axis=axis, concat_axis=axis, tiled=True)  17.8 us
    all_gather x1, blocking collectives, gather_weight(): first = lax.all_gather(value_weight, 'ay', axis=1, tiled=True)  13.3 us
    all_to_all x2, waiting for transfers between devices, exchange(): lax.all_to_all(x, 'az', split_axis=axis + 1, concat_axis=axis + 1, tiled=...  9.86 us
    all_to_all x2, starting transfers between devices, exchange(): x = lax.all_to_all(x, 'ay', split_axis=axis, concat_axis=axis, tiled=True)  9.46 us
  transfers between devices with their start and end apart: 6, of which 4 were waited for; matrix products, arithmetic and copies ran while one was open for 12% of the time, Pallas kernels for 0%

profile of v5, /device:TPU:32, one launch (start us, length us, event | category | flops | bytes accessed | tf_op | source)
XLA Modules:
  0.0 185.4 jit_solution(11392342312017862404)
XLA Ops:
  8.2 1.5 gather_fusion.1
  9.7 1.4 copy.92
  12.7 1.2 copy.93
  13.8 15.3 %all-to-all-start = ((bf16[4,16,3,1152]{3,0,2,1:T(4,128)(2,1)}), bf16[4,16,3,1152]{3,0,2,1:T(4,128)(2,1)S(1)}, u32[]{:S(2)}, u32[]{:S(2)}) async-start(bf16[4,16,3,1152]{3,0,2,1:T(4,128)(2,1)} %copy.93), calls=%async_computation.1 | async-start | bytes 884736 | tf_op jit(solution)/shard_map/all_to_all | solution.py:46
  29.2 13.3 %all_gather.9 = bf16[1024,64]{0,1:T(8,128)(2,1)} all-gather(bf16[1024,16]{0,1:T(8,128)(2,1)S(1)} %copy-done.10), channel_id=1, replica_groups=mesh['ay'=4,'az'=16,'mp'=8] {'ay'}, dimensions={1}, use_global_device_ids=true | all-gather | bytes 163840 | tf_op jit(solution)/shard_map/all_gather | solution.py:35
  42.6 9.9 %all-to-all-done = bf16[4,16,3,1152]{3,0,2,1:T(4,128)(2,1)S(1)} async-done(((bf16[4,16,3,1152]{3,0,2,1:T(4,128)(2,1)}), bf16[4,16,3,1152]{3,0,2,1:T(4,128)(2,1)S(1)}, u32[]{:S(2)}, u32[]{:S(2)}) %all-to-all-start) | async-done | bytes 442400 | tf_op jit(solution)/shard_map/all_to_all | solution.py:46
  53.3 4.5 %all-to-all-start.1 = ((bf16[4,16,3,1152]{3,1,2,0:T(8,128)(2,1)}), bf16[4,16,3,1152]{3,1,2,0:T(8,128)(2,1)S(1)}, u32[]{:S(2)}, u32[]{:S(2)}) async-start(bf16[4,16,3,1152]{3,1,2,0:T(8,128)(2,1)} %copy.94), calls=%async_computation.2 | async-start | bytes 884736 | tf_op jit(solution)/shard_map/all_to_all | solution.py:47
  57.9 7.4 %all-to-all-done.1 = bf16[4,16,3,1152]{3,1,2,0:T(8,128)(2,1)S(1)} async-done(((bf16[4,16,3,1152]{3,1,2,0:T(8,128)(2,1)}), bf16[4,16,3,1152]{3,1,2,0:T(8,128)(2,1)S(1)}, u32[]{:S(2)}, u32[]{:S(2)}) %all-to-all-start.1) | async-done | bytes 442400 | tf_op jit(solution)/shard_map/all_to_all | solution.py:47
  66.6 25.5 %all-reduce.2 = (bf16[3,128,64]{1,2,0:T(8,128)(2,1)S(1)}, bf16[3,128,64]{1,2,0:T(8,128)(2,1)S(1)}) all-reduce(f32[3,128,64]{1,2,0:T(8,128)S(1)} %convolution_bitcast_fusion.1, f32[3,128,64]{1,2,0:T(8,128)S(1)} %convolution_multiply_fusion.2), channel_id=1, replica_groups=mesh['ay'=4,'az'=16,'mp'=8] {'mp'}, use_global_device_ids=true, to_apply=%region_2.3 | all-reduce | flops 49152 | bytes 294912 | tf_op jit(solution)/shard_map/psum | solution.py:117
  93.3 1.6 copy.98
  94.9 1.3 concatenate.19
  96.3 1.2 pad_maximum_fusion
  97.6 1.3 copy.99
  98.8 10.4 %all-to-all-start.2 = ((f32[3,4,16,1,1152]{4,1,0,3,2:T(4,128)}), f32[3,4,16,1,1152]{4,1,0,3,2:T(4,128)S(1)}, u32[]{:S(2)}, u32[]{:S(2)}) async-start(f32[3,4,16,1,1152]{4,1,0,3,2:T(4,128)} %copy.99), calls=%async_computation.3 | async-start | bytes 1769472 | tf_op jit(solution)/shard_map/all_to_all | solution.py:46
  109.3 18.7 %all-gather.2.cloned.1.call-done = bf16[1024,1024]{0,1:T(8,128)(2,1)} async-done(((bf16[1024,64]{0,1:T(8,128)(2,1)}), bf16[1024,1024]{0,1:T(8,128)(2,1)}) %all-gather.2.cloned.1.call-update) | async-done | bytes 2097168 | tf_op jit(solution)/shard_map/all_gather | solution.py:36
  127.9 1.8 copy.91
  129.7 1.3 copy-done.2
  131.0 2.2 %fusion.21 = f32[384,1024]{1,0:T(8,128)} fusion(bf16[384,1024]{1,0:T(8,128)(2,1)S(1)} %copy-done, bf16[1024,1024]{0,1:T(8,128)(2,1)S(1)} %bitcast.78), kind=kOutput, calls=%fused_computation.45 | convolution fusion | flops 805306368 | bytes 4456448 | tf_op jit(solution)/shard_map/dot_general | solution.py:108
  133.2 19.3 %all_gather.11 = bf16[384,1024]{1,0:T(8,128)(2,1)} all-gather(bf16[384,128]{1,0:T(8,128)(2,1)S(1)} %broadcast_multiply_fusion), channel_id=1, replica_groups=mesh['ay'=4,'az'=16,'mp'=8] {'mp'}, dimensions={1}, use_global_device_ids=true | all-gather | bytes 884736 | tf_op jit(solution)/shard_map/all_gather | solution.py:90
  153.5 5.0 %all-to-all-start.3 = ((f32[3,4,16,1,1152]{4,2,0,3,1:T(8,128)}), f32[3,4,16,1,1152]{4,2,0,3,1:T(8,128)S(1)}, u32[]{:S(2)}, u32[]{:S(2)}) async-start(f32[3,4,16,1,1152]{4,2,0,3,1:T(8,128)} %copy.100), calls=%async_computation.4 | async-start | bytes 1769472 | tf_op jit(solution)/shard_map/all_to_all | solution.py:47
  160.1 1.9 %fusion = bf16[384,1024]{1,0:T(8,128)(2,1)} fusion(f32[3,128,1024]{2,1,0:T(8,128)S(1)} %fusion.22, bf16[384,1024]{1,0:T(8,128)(2,1)S(1)} %copy-done.6, bf16[1024,1024]{0,1:T(8,128)(2,1)S(1)} %bitcast.79), kind=kOutput, calls=%fused_computation.3 | convolution fusion | flops 806092800 | bytes 5242880 | tf_op jit(solution)/shard_map/dot_general | solution.py:130
  162.0 10.3 %all-to-all-done.3 = f32[3,4,16,1,1152]{4,2,0,3,1:T(8,128)S(1)} async-done(((f32[3,4,16,1,1152]{4,2,0,3,1:T(8,128)}), f32[3,4,16,1,1152]{4,2,0,3,1:T(8,128)S(1)}, u32[]{:S(2)}, u32[]{:S(2)}) %all-to-all-start.3) | async-done | bytes 884768 | tf_op jit(solution)/shard_map/all_to_all | solution.py:47
  175.5 1.4 divide_subtract_fusion
  176.9 1.7 fusion.5
  (59 shorter events, 11.9 us)
Async XLA Ops:
  7.2 58.8 %copy-start = (bf16[384,1024]{1,0:T(8,128)(2,1)S(1)}, bf16[384,1024]{1,0:T(8,128)(2,1)}, u32[]{:S(2)}) copy-start(bf16[384,1024]{1,0:T(8,128)(2,1)} %param.12) | copy-start | bytes 2359300
  12.4 16.9 %copy-start.10 = (bf16[1024,16]{0,1:T(8,128)(2,1)S(1)}, bf16[1024,16]{0,1:T(8,128)(2,1)}, u32[]{:S(2)}) copy-start(bf16[1024,16]{0,1:T(8,128)(2,1)} %param.14) | copy-start | bytes 98308
  12.4 30.2 %copy-start.13 = (s32[192]{0:T(256)S(1)}, s32[192]{0:T(256)}, u32[]{:S(2)}) copy-start(s32[192]{0:T(256)} %param.22) | copy-start | bytes 2308
  13.8 44.0 %copy-start.9 = (bf16[384,128]{1,0:T(8,128)(2,1)S(1)}, bf16[384,128]{1,0:T(8,128)(2,1)}, u32[]{:S(2)}) copy-start(bf16[384,128]{1,0:T(8,128)(2,1)} %param.13) | copy-start | bytes 294916
  13.8 38.6 %all-to-all-start = ((bf16[4,16,3,1152]{3,0,2,1:T(4,128)(2,1)}), bf16[4,16,3,1152]{3,0,2,1:T(4,128)(2,1)S(1)}, u32[]{:S(2)}, u32[]{:S(2)}) async-start(bf16[4,16,3,1152]{3,0,2,1:T(4,128)(2,1)} %copy.93), calls=%async_computation.1 | async-start | bytes 884736 | tf_op jit(solution)/shard_map/all_to_all | solution.py:46
  29.2 98.8 %all-gather.2.cloned.1.call-start = ((), (), s32[]{:S(2)}) async-start(), calls=%async_computation.5 | async-start | bytes 2228224 | tf_op jit(solution)/shard_map/all_gather | solution.py:36
  53.3 12.1 %all-to-all-start.1 = ((bf16[4,16,3,1152]{3,1,2,0:T(8,128)(2,1)}), bf16[4,16,3,1152]{3,1,2,0:T(8,128)(2,1)S(1)}, u32[]{:S(2)}, u32[]{:S(2)}) async-start(bf16[4,16,3,1152]{3,1,2,0:T(8,128)(2,1)} %copy.94), calls=%async_computation.2 | async-start | bytes 884736 | tf_op jit(solution)/shard_map/all_to_all | solution.py:47
  65.4 1.0 copy-start.4
  98.8 53.7 %all-to-all-start.2 = ((f32[3,4,16,1,1152]{4,1,0,3,2:T(4,128)}), f32[3,4,16,1,1152]{4,1,0,3,2:T(4,128)S(1)}, u32[]{:S(2)}, u32[]{:S(2)}) async-start(f32[3,4,16,1,1152]{4,1,0,3,2:T(4,128)} %copy.99), calls=%async_computation.3 | async-start | bytes 1769472 | tf_op jit(solution)/shard_map/all_to_all | solution.py:46
  109.2 67.7 %reduce-scatter.2.cloned.1.call-start = ((), (), s32[]{:S(2)}) async-start(), calls=%async_computation.6 | async-start | bytes 1769472 | tf_op jit(solution)/shard_map/reduce_scatter | solution.py:113
  129.7 1.3 copy-start.2
  153.5 6.6 %copy-start.6 = (bf16[384,1024]{1,0:T(8,128)(2,1)S(1)}, bf16[384,1024]{1,0:T(8,128)(2,1)}, u32[]{:S(2)}) copy-start(bf16[384,1024]{1,0:T(8,128)(2,1)} %all_gather.11) | copy-start | bytes 2359300
  153.5 18.8 %all-to-all-start.3 = ((f32[3,4,16,1,1152]{4,2,0,3,1:T(8,128)}), f32[3,4,16,1,1152]{4,2,0,3,1:T(8,128)S(1)}, u32[]{:S(2)}, u32[]{:S(2)}) async-start(f32[3,4,16,1,1152]{4,2,0,3,1:T(8,128)} %copy.100), calls=%async_computation.4 | async-start | bytes 1769472 | tf_op jit(solution)/shard_map/all_to_all | solution.py:47
  158.5 1.6 copy-start.3
  172.4 1.1 copy-start.1
  172.4 1.1 copy-start.11
  172.4 1.1 copy-start.12
  173.0 2.5 %copy-start.5 = (bf16[128,1,16,64]{0,3,2,1:T(8,128)(2,1)S(1)}, bf16[128,1,16,64]{0,3,2,1:T(8,128)(2,1)}, u32[]{:S(2)}) copy-start(bf16[128,1,16,64]{0,3,2,1:T(8,128)(2,1)} %param.15) | copy-start | bytes 786436
  173.5 2.0 %copy-start.7 = (f32[128,1,16,64]{0,3,2,1:T(8,128)S(1)}, f32[128,1,16,64]{0,3,2,1:T(8,128)}, u32[]{:S(2)}) copy-start(f32[128,1,16,64]{0,3,2,1:T(8,128)} %param.16) | copy-start | bytes 1572868
  173.5 2.0 %copy-start.8 = (f32[128,1,16,64]{0,3,2,1:T(8,128)S(1)}, f32[128,1,16,64]{0,3,2,1:T(8,128)}, u32[]{:S(2)}) copy-start(f32[128,1,16,64]{0,3,2,1:T(8,128)} %param.17) | copy-start | bytes 1572868
Sparse Core Ops, SparseCore 0:
  42.6 85.2 all-gather.1
  133.3 39.7 reduce-scatter.1

commit v6 on v5

--- a/solution.py
+++ b/solution.py
@@ -103,7 +103,7 @@
         .reshape(tiles_here, n_adapter * row_part, rank)
     )
     up_panel = arrived[:, :, row_part * rank :].transpose(1, 0, 2)
-    w_full = gather_weight(value_weight)
+    w_full, masked_full = lax.optimization_barrier((gather_weight(value_weight), masked_full))
     token_tiles = tokens.reshape(tiles_here, TILE, feat_part)
     frozen_part = jnp.dot(
         tokens,

time: 186 us -> 182 us (0.978)
  the two profiles are of different devices: /device:TPU:32 before, /device:TPU:6 now
where the time goes in v6:
time: 182 us; the launch traced here: 181 us
  blocking collectives  51.4 us (28%)
  waiting for transfers between devices  50.6 us (28%)
  starting transfers between devices  30.7 us (17%)
  local copies, waits for them, and re-layouts  19 us (10%)
  between operations  14.4 us (8%)
  matrix products  9.62 us (5%)
  other arithmetic  4.96 us (3%)
    all_to_all x2, waiting for transfers between devices, exchange(): lax.all_to_all(x, 'az', split_axis=axis + 1, concat_axis=axis + 1, tiled=...  31.7 us
    psum x1, blocking collectives, shards(): down_sum = lax.psum(down_part, 'mp')  23.1 us
    all_to_all x2, starting transfers between devices, exchange(): lax.all_to_all(x, 'az', split_axis=axis + 1, concat_axis=axis + 1, tiled=...  22.4 us
    all_gather x1, blocking collectives, shards(): masked_full = lax.all_gather(masked_own, 'mp', axis=1, tiled=True)  15.1 us
    all_gather x1, blocking collectives, gather_weight(): first = lax.all_gather(value_weight, 'ay', axis=1, tiled=True)  13.3 us
    all_to_all x2, waiting for transfers between devices, exchange(): x = lax.all_to_all(x, 'ay', split_axis=axis, concat_axis=axis, tiled=True)  12.6 us
    all_to_all x2, starting transfers between devices, exchange(): x = lax.all_to_all(x, 'ay', split_axis=axis, concat_axis=axis, tiled=True)  8.26 us
    all_gather x1, waiting for transfers between devices, gather_weight(): whole = lax.all_gather(first, 'az', axis=1, tiled=True)  6.22 us
  transfers between devices with their start and end apart: 6, of which 5 were waited for; matrix products, arithmetic and copies ran while one was open for 13% of the time, Pallas kernels for 0%

profile of v6, /device:TPU:6, one launch (start us, length us, event | category | flops | bytes accessed | tf_op | source)
XLA Modules:
  0.0 180.8 jit_solution(1070229916437559906)
XLA Ops:
  8.2 1.5 gather_fusion.1
  9.7 1.4 copy.102
  13.8 15.3 %all-to-all-start = ((bf16[4,16,3,1152]{3,0,2,1:T(4,128)(2,1)}), bf16[4,16,3,1152]{3,0,2,1:T(4,128)(2,1)S(1)}, u32[]{:S(2)}, u32[]{:S(2)}) async-start(bf16[4,16,3,1152]{3,0,2,1:T(4,128)(2,1)} %copy.103), calls=%async_computation.1 | async-start | bytes 884736 | tf_op jit(solution)/shard_map/all_to_all | solution.py:46
  29.2 13.3 %all_gather.9 = bf16[1024,64]{0,1:T(8,128)(2,1)} all-gather(bf16[1024,16]{0,1:T(8,128)(2,1)S(1)} %copy-done.11), channel_id=1, replica_groups=mesh['ay'=4,'az'=16,'mp'=8] {'ay'}, dimensions={1}, use_global_device_ids=true | all-gather | bytes 163840 | tf_op jit(solution)/shard_map/all_gather | solution.py:35
  42.6 12.6 %all-to-all-done = bf16[4,16,3,1152]{3,0,2,1:T(4,128)(2,1)S(1)} async-done(((bf16[4,16,3,1152]{3,0,2,1:T(4,128)(2,1)}), bf16[4,16,3,1152]{3,0,2,1:T(4,128)(2,1)S(1)}, u32[]{:S(2)}, u32[]{:S(2)}) %all-to-all-start) | async-done | bytes 442400 | tf_op jit(solution)/shard_map/all_to_all | solution.py:46
  56.0 4.5 %all-to-all-start.1 = ((bf16[4,16,3,1152]{3,1,2,0:T(8,128)(2,1)}), bf16[4,16,3,1152]{3,1,2,0:T(8,128)(2,1)S(1)}, u32[]{:S(2)}, u32[]{:S(2)}) async-start(bf16[4,16,3,1152]{3,1,2,0:T(8,128)(2,1)} %copy.104), calls=%async_computation.2 | async-start | bytes 884736 | tf_op jit(solution)/shard_map/all_to_all | solution.py:47
  60.7 7.4 %all-to-all-done.1 = bf16[4,16,3,1152]{3,1,2,0:T(8,128)(2,1)S(1)} async-done(((bf16[4,16,3,1152]{3,1,2,0:T(8,128)(2,1)}), bf16[4,16,3,1152]{3,1,2,0:T(8,128)(2,1)S(1)}, u32[]{:S(2)}, u32[]{:S(2)}) %all-to-all-start.1) | async-done | bytes 442400 | tf_op jit(solution)/shard_map/all_to_all | solution.py:47
  69.3 23.1 %all-reduce.2 = (bf16[3,128,64]{1,2,0:T(8,128)(2,1)S(1)}, bf16[3,128,64]{1,2,0:T(8,128)(2,1)S(1)}) all-reduce(f32[3,128,64]{1,2,0:T(8,128)S(1)} %convolution_bitcast_fusion.2, f32[3,128,64]{1,2,0:T(8,128)S(1)} %convolution_multiply_fusion.2), channel_id=1, replica_groups=mesh['ay'=4,'az'=16,'mp'=8] {'mp'}, use_global_device_ids=true, to_apply=%region_2.3 | all-reduce | flops 49152 | bytes 294912 | tf_op jit(solution)/shard_map/psum | solution.py:117
  93.6 1.6 copy.109
  95.2 1.3 concatenate.19
  96.6 1.2 pad_maximum_fusion
  97.9 1.3 copy.110
  99.1 7.0 %all-to-all-start.2 = ((f32[3,4,16,1,1152]{4,1,0,3,2:T(4,128)}), f32[3,4,16,1,1152]{4,1,0,3,2:T(4,128)S(1)}, u32[]{:S(2)}, u32[]{:S(2)}) async-start(f32[3,4,16,1,1152]{4,1,0,3,2:T(4,128)} %copy.110), calls=%async_computation.3 | async-start | bytes 1769472 | tf_op jit(solution)/shard_map/all_to_all | solution.py:46
  106.2 15.1 %all_gather.11 = bf16[384,1024]{1,0:T(8,128)(2,1)} all-gather(bf16[384,128]{1,0:T(8,128)(2,1)S(1)} %broadcast_multiply_fusion), channel_id=1, replica_groups=mesh['ay'=4,'az'=16,'mp'=8] {'mp'}, dimensions={1}, use_global_device_ids=true | all-gather | bytes 884736 | tf_op jit(solution)/shard_map/all_gather | solution.py:90
  121.3 6.2 %all-gather.2.cloned.1.call-done = bf16[1024,1024]{0,1:T(8,128)(2,1)} async-done(((bf16[1024,64]{0,1:T(8,128)(2,1)}), bf16[1024,1024]{0,1:T(8,128)(2,1)}) %all-gather.2.cloned.1.call-update) | async-done | bytes 2097168 | tf_op jit(solution)/shard_map/all_gather | solution.py:36
  127.5 1.8 copy.101
  129.3 1.3 copy-done.2
  130.6 2.4 %convolution_bitcast_fusion = f32[384,1024]{0,1:T(8,128)} fusion(bf16[1024,1024]{0,1:T(8,128)(2,1)S(1)} %bitcast.75, bf16[384,1024]{1,0:T(8,128)(2,1)S(1)} %copy-done), kind=kOutput, calls=%fused_computation.4 | convolution fusion | flops 805306368 | bytes 4456448 | tf_op jit(solution)/shard_map/dot_general | solution.py:108
  133.1 19.2 %all-to-all-done.2 = f32[3,4,16,1,1152]{4,1,0,3,2:T(4,128)S(1)} async-done(((f32[3,4,16,1,1152]{4,1,0,3,2:T(4,128)}), f32[3,4,16,1,1152]{4,1,0,3,2:T(4,128)S(1)}, u32[]{:S(2)}, u32[]{:S(2)}) %all-to-all-start.2) | async-done | bytes 884768 | tf_op jit(solution)/shard_map/all_to_all | solution.py:46
  153.2 3.8 %all-to-all-start.3 = ((f32[3,4,16,1,1152]{4,2,0,3,1:T(8,128)}), f32[3,4,16,1,1152]{4,2,0,3,1:T(8,128)S(1)}, u32[]{:S(2)}, u32[]{:S(2)}) async-start(f32[3,4,16,1,1152]{4,2,0,3,1:T(8,128)} %copy.111), calls=%async_computation.4 | async-start | bytes 1769472 | tf_op jit(solution)/shard_map/all_to_all | solution.py:47
  159.4 1.2 copy-done.3
  160.6 1.9 %fusion = bf16[384,1024]{1,0:T(8,128)(2,1)} fusion(f32[3,128,1024]{2,1,0:T(8,128)S(1)} %fusion.19, bf16[384,1024]{1,0:T(8,128)(2,1)S(1)} %copy-done.6, bf16[1024,1024]{0,1:T(8,128)(2,1)S(1)} %bitcast.76), kind=kOutput, calls=%fused_computation.3 | convolution fusion | flops 806092800 | bytes 5242880 | tf_op jit(solution)/shard_map/dot_general | solution.py:130
  162.4 5.2 %all-to-all-done.3 = f32[3,4,16,1,1152]{4,2,0,3,1:T(8,128)S(1)} async-done(((f32[3,4,16,1,1152]{4,2,0,3,1:T(8,128)}), f32[3,4,16,1,1152]{4,2,0,3,1:T(8,128)S(1)}, u32[]{:S(2)}, u32[]{:S(2)}) %all-to-all-start.3) | async-done | bytes 884768 | tf_op jit(solution)/shard_map/all_to_all | solution.py:47
  170.8 1.4 divide_subtract_fusion
  (63 shorter events, 15.5 us)
Async XLA Ops:
  7.2 61.5 %copy-start = (bf16[384,1024]{1,0:T(8,128)(2,1)S(1)}, bf16[384,1024]{1,0:T(8,128)(2,1)}, u32[]{:S(2)}) copy-start(bf16[384,1024]{1,0:T(8,128)(2,1)} %param.12) | copy-start | bytes 2359300
  12.4 16.9 %copy-start.11 = (bf16[1024,16]{0,1:T(8,128)(2,1)S(1)}, bf16[1024,16]{0,1:T(8,128)(2,1)}, u32[]{:S(2)}) copy-start(bf16[1024,16]{0,1:T(8,128)(2,1)} %param.14) | copy-start | bytes 98308
  12.4 30.2 %copy-start.14 = (s32[192]{0:T(256)S(1)}, s32[192]{0:T(256)}, u32[]{:S(2)}) copy-start(s32[192]{0:T(256)} %param.22) | copy-start | bytes 2308
  13.8 46.7 %copy-start.10 = (bf16[384,128]{1,0:T(8,128)(2,1)S(1)}, bf16[384,128]{1,0:T(8,128)(2,1)}, u32[]{:S(2)}) copy-start(bf16[384,128]{1,0:T(8,128)(2,1)} %param.13) | copy-start | bytes 294916
  13.8 41.3 %all-to-all-start = ((bf16[4,16,3,1152]{3,0,2,1:T(4,128)(2,1)}), bf16[4,16,3,1152]{3,0,2,1:T(4,128)(2,1)S(1)}, u32[]{:S(2)}, u32[]{:S(2)}) async-start(bf16[4,16,3,1152]{3,0,2,1:T(4,128)(2,1)} %copy.103), calls=%async_computation.1 | async-start | bytes 884736 | tf_op jit(solution)/shard_map/all_to_all | solution.py:46
  29.2 98.4 %all-gather.2.cloned.1.call-start = ((), (), s32[]{:S(2)}) async-start(), calls=%async_computation.5 | async-start | bytes 2228224 | tf_op jit(solution)/shard_map/all_gather | solution.py:36
  56.0 12.1 %all-to-all-start.1 = ((bf16[4,16,3,1152]{3,1,2,0:T(8,128)(2,1)}), bf16[4,16,3,1152]{3,1,2,0:T(8,128)(2,1)S(1)}, u32[]{:S(2)}, u32[]{:S(2)}) async-start(bf16[4,16,3,1152]{3,1,2,0:T(8,128)(2,1)} %copy.104), calls=%async_computation.2 | async-start | bytes 884736 | tf_op jit(solution)/shard_map/all_to_all | solution.py:47
  68.2 1.0 copy-start.4
  99.1 53.1 %all-to-all-start.2 = ((f32[3,4,16,1,1152]{4,1,0,3,2:T(4,128)}), f32[3,4,16,1,1152]{4,1,0,3,2:T(4,128)S(1)}, u32[]{:S(2)}, u32[]{:S(2)}) async-start(f32[3,4,16,1,1152]{4,1,0,3,2:T(4,128)} %copy.110), calls=%async_computation.3 | async-start | bytes 1769472 | tf_op jit(solution)/shard_map/all_to_all | solution.py:46
  106.2 66.1 %reduce-scatter.2.cloned.1.call-start = ((), (), s32[]{:S(2)}) async-start(), calls=%async_computation.6 | async-start | bytes 1769472 | tf_op jit(solution)/shard_map/reduce_scatter | solution.py:113
  129.3 1.3 copy-start.2
  153.2 14.4 %all-to-all-start.3 = ((f32[3,4,16,1,1152]{4,2,0,3,1:T(8,128)}), f32[3,4,16,1,1152]{4,2,0,3,1:T(8,128)S(1)}, u32[]{:S(2)}, u32[]{:S(2)}) async-start(f32[3,4,16,1,1152]{4,2,0,3,1:T(8,128)} %copy.111), calls=%async_computation.4 | async-start | bytes 1769472 | tf_op jit(solution)/shard_map/all_to_all | solution.py:47
  157.0 2.4 %copy-start.6 = (bf16[384,1024]{1,0:T(8,128)(2,1)S(1)}, bf16[384,1024]{1,0:T(8,128)(2,1)}, u32[]{:S(2)}) copy-start(bf16[384,1024]{1,0:T(8,128)(2,1)} %all_gather.11) | copy-start | bytes 2359300
  158.9 1.6 copy-start.3
  167.7 1.1 copy-start.1
  167.7 1.1 copy-start.12
  167.7 1.1 copy-start.13
  168.3 2.5 %copy-start.5 = (bf16[128,1,16,64]{0,3,2,1:T(8,128)(2,1)S(1)}, bf16[128,1,16,64]{0,3,2,1:T(8,128)(2,1)}, u32[]{:S(2)}) copy-start(bf16[128,1,16,64]{0,3,2,1:T(8,128)(2,1)} %param.15) | copy-start | bytes 786436
  168.8 2.0 %copy-start.8 = (f32[128,1,16,64]{0,3,2,1:T(8,128)S(1)}, f32[128,1,16,64]{0,3,2,1:T(8,128)}, u32[]{:S(2)}) copy-start(f32[128,1,16,64]{0,3,2,1:T(8,128)} %param.16) | copy-start | bytes 1572868
  168.8 2.0 %copy-start.9 = (f32[128,1,16,64]{0,3,2,1:T(8,128)S(1)}, f32[128,1,16,64]{0,3,2,1:T(8,128)}, u32[]{:S(2)}) copy-start(f32[128,1,16,64]{0,3,2,1:T(8,128)} %param.17) | copy-start | bytes 1572868
  170.8 1.4 copy-start.7
Sparse Core Ops, SparseCore 0:
  42.6 84.8 all-gather.1
  133.2 36.8 reduce-scatter.1

commit v7 on v6

--- a/solution.py
+++ b/solution.py
@@ -26,6 +26,11 @@
 
 
 ADAPTER = ("ay", "az")
+MP = ("mx", "mc")
+
+
+def sum_over_mp(x):
+    return lax.psum(lax.psum(x, "mc"), "mx")
 
 
 def gather_weight(value_weight):
@@ -57,7 +62,15 @@
         n_y = 1
     if n_y < 1 or n_adapter % n_y:
         n_y = 1
-    return Mesh(devices.reshape(n_y, n_adapter // n_y, devices.shape[1]), ("ay", "az", "mp"))
+    n_mp = devices.shape[1]
+    try:
+        n_c = len({d.core_on_chip for d in devices[0, :]})
+    except (AttributeError, TypeError):
+        n_c = 1
+    if n_c < 1 or n_mp % n_c:
+        n_c = 1
+    shape = (n_y, n_adapter // n_y, n_mp // n_c, n_c)
+    return Mesh(devices.reshape(shape), ("ay", "az", "mx", "mc"))
 
 
 def shards(
@@ -87,7 +100,7 @@
     my_lengths = lax.dynamic_slice_in_dim(tile_length, my_index * tiles_here, tiles_here)
     active_rows = (jnp.arange(TILE)[None, :] < my_lengths[:, None]).reshape(tok_count, 1)
     masked_own = cotangent * active_rows.astype(jnp.bfloat16)
-    masked_full = lax.all_gather(masked_own, "mp", axis=1, tiled=True)
+    masked_full = lax.all_gather(masked_own, MP, axis=1, tiled=True)
     n_adapter = tile_total // tiles_here
     row_part = down_store.shape[2]
     rank = down_store.shape[3]
@@ -110,11 +123,11 @@
         w_full,
         preferred_element_type=jnp.float32,
     )
-    frozen_local = lax.psum_scatter(frozen_part, "mp", scatter_dimension=1, tiled=True)
+    frozen_local = lax.psum_scatter(frozen_part, MP, scatter_dimension=1, tiled=True)
     down_part = jnp.einsum(
         "ntd,ndr->ntr", token_tiles, down_panel, preferred_element_type=jnp.float32
     )
-    down_sum = lax.psum(down_part, "mp")
+    down_sum = sum_over_mp(down_part)
     down_portion = down_sum.astype(jnp.bfloat16)
     adapter_term = jnp.einsum(
         "ntr,nrv->ntv", down_portion, up_panel, preferred_element_type=jnp.float32
@@ -126,7 +139,7 @@
     backward_piece = adapter_scale * jnp.einsum(
         "ntv,nrv->ntr", tile_mask, up_panel, preferred_element_type=jnp.float32
     )
-    backward_portion = lax.psum(backward_piece, "mp").astype(jnp.bfloat16)
+    backward_portion = sum_over_mp(backward_piece).astype(jnp.bfloat16)
     frozen_backward = lax.dot_general(
         masked_full,
         w_full,
@@ -175,15 +188,15 @@
 def solution(mesh):
     mesh = split_adapter(mesh)
     placed = (
-        P(ADAPTER, "mp"),
-        P(ADAPTER, "mp"),
-        P("mp", ADAPTER),
-        P(None, "mp", ADAPTER, None),
-        P(None, "mp", ADAPTER, None),
-        P(None, "mp", ADAPTER, None),
-        P(None, ADAPTER, "mp"),
-        P(None, ADAPTER, "mp"),
-        P(None, ADAPTER, "mp"),
+        P(ADAPTER, MP),
+        P(ADAPTER, MP),
+        P(MP, ADAPTER),
+        P(None, MP, ADAPTER, None),
+        P(None, MP, ADAPTER, None),
+        P(None, MP, ADAPTER, None),
+        P(None, ADAPTER, MP),
+        P(None, ADAPTER, MP),
+        P(None, ADAPTER, MP),
         P(),
         P(),
         P(),
@@ -193,14 +206,14 @@
         mesh=mesh,
         in_specs=placed,
         out_specs=(
-            P(ADAPTER, "mp"),
-            P(ADAPTER, "mp"),
-            P(None, "mp", ADAPTER, None),
-            P(None, "mp", ADAPTER, None),
-            P(None, "mp", ADAPTER, None),
-            P(None, ADAPTER, "mp"),
-            P(None, ADAPTER, "mp"),
-            P(None, ADAPTER, "mp"),
+            P(ADAPTER, MP),
+            P(ADAPTER, MP),
+            P(None, MP, ADAPTER, None),
+            P(None, MP, ADAPTER, None),
+            P(None, MP, ADAPTER, None),
+            P(None, ADAPTER, MP),
+            P(None, ADAPTER, MP),
+            P(None, ADAPTER, MP),
         ),
         check_vma=False,
     )

time: 182 us -> 218 us (1.20); the launches traced: 181 us -> 214 us
  waiting for transfers between devices: 50.6 us -> 82 us
  blocking collectives: 51.4 us -> 45 us
  starting transfers between devices: 30.7 us -> 36.2 us
    psum x0 -> x1, waiting for transfers between devices: none -> 20.3 us  [sum_over_mp(): return lax.psum(lax.psum(x, 'mc'), 'mx')]
    all_to_all x2, waiting for transfers between devices: 31.7 us -> 39.3 us  [exchange(): lax.all_to_all(x, 'az', split_axis=axis + 1, concat_axis=axis + 1, tiled=...]
    psum x1, blocking collectives: 23.1 us -> 17.2 us  [sum_over_mp(): return lax.psum(lax.psum(x, 'mc'), 'mx')]
    all_to_all x2, starting transfers between devices: 22.4 us -> 27.5 us  [exchange(): lax.all_to_all(x, 'az', split_axis=axis + 1, concat_axis=axis + 1, tiled=...]
    all_gather x1, waiting for transfers between devices: 6.22 us -> 8.68 us  [gather_weight(): whole = lax.all_gather(first, 'az', axis=1, tiled=True)]
  transfers between devices with their start and end apart: 6 -> 7, of which waited for: 5 -> 7; matrix products, arithmetic and copies ran while one was open for 13% -> 10% of each run, Pallas kernels for 0% -> 0%
where the time goes in v7:
time: 218 us; the launch traced here: 214 us
  waiting for transfers between devices  82 us (38%)
  blocking collectives  45 us (21%)
  starting transfers between devices  36.2 us (17%)
  local copies, waits for them, and re-layouts  19 us (9%)
  between operations  15.8 us (7%)
  matrix products  10.9 us (5%)
  other arithmetic  4.97 us (2%)
    all_to_all x2, waiting for transfers between devices, exchange(): lax.all_to_all(x, 'az', split_axis=axis + 1, concat_axis=axis + 1, tiled=...  39.3 us
    all_to_all x2, starting transfers between devices, exchange(): lax.all_to_all(x, 'az', split_axis=axis + 1, concat_axis=axis + 1, tiled=...  27.5 us
    psum x1, waiting for transfers between devices, sum_over_mp(): return lax.psum(lax.psum(x, 'mc'), 'mx')  20.3 us
    psum x1, blocking collectives, sum_over_mp(): return lax.psum(lax.psum(x, 'mc'), 'mx')  17.2 us
    all_gather x1, blocking collectives, shards(): masked_full = lax.all_gather(masked_own, MP, axis=1, tiled=True)  15 us
    all_gather x1, blocking collectives, gather_weight(): first = lax.all_gather(value_weight, 'ay', axis=1, tiled=True)  12.7 us
    all_to_all x2, waiting for transfers between devices, exchange(): x = lax.all_to_all(x, 'ay', split_axis=axis, concat_axis=axis, tiled=True)  12.3 us
    all_gather x1, waiting for transfers between devices, gather_weight(): whole = lax.all_gather(first, 'az', axis=1, tiled=True)  8.68 us
  transfers between devices with their start and end apart: 7, of which 7 were waited for; matrix products, arithmetic and copies ran while one was open for 10% of the time, Pallas kernels for 0%

profile of v7, /device:TPU:6, one launch (start us, length us, event | category | flops | bytes accessed | tf_op | source)
XLA Modules:
  0.0 213.9 jit_solution(15051298971881083999)
XLA Ops:
  9.0 1.5 gather_fusion.1
  10.5 1.4 copy.102
  14.7 15.3 %all-to-all-start = ((bf16[4,16,3,1152]{3,0,2,1:T(4,128)(2,1)}), bf16[4,16,3,1152]{3,0,2,1:T(4,128)(2,1)S(1)}, u32[]{:S(2)}, u32[]{:S(2)}) async-start(bf16[4,16,3,1152]{3,0,2,1:T(4,128)(2,1)} %copy.103), calls=%async_computation.1 | async-start | bytes 884736 | tf_op jit(solution)/shard_map/all_to_all | solution.py:51
  30.1 25.9 %all-to-all-done = bf16[4,16,3,1152]{3,0,2,1:T(4,128)(2,1)S(1)} async-done(((bf16[4,16,3,1152]{3,0,2,1:T(4,128)(2,1)}), bf16[4,16,3,1152]{3,0,2,1:T(4,128)(2,1)S(1)}, u32[]{:S(2)}, u32[]{:S(2)}) %all-to-all-start) | async-done | bytes 442400 | tf_op jit(solution)/shard_map/all_to_all | solution.py:51
  56.8 4.5 %all-to-all-start.1 = ((bf16[4,16,3,1152]{3,1,2,0:T(8,128)(2,1)}), bf16[4,16,3,1152]{3,1,2,0:T(8,128)(2,1)S(1)}, u32[]{:S(2)}, u32[]{:S(2)}) async-start(bf16[4,16,3,1152]{3,1,2,0:T(8,128)(2,1)} %copy.104), calls=%async_computation.2 | async-start | bytes 884736 | tf_op jit(solution)/shard_map/all_to_all | solution.py:52
  61.5 7.7 %all-to-all-done.1 = bf16[4,16,3,1152]{3,1,2,0:T(8,128)(2,1)S(1)} async-done(((bf16[4,16,3,1152]{3,1,2,0:T(8,128)(2,1)}), bf16[4,16,3,1152]{3,1,2,0:T(8,128)(2,1)S(1)}, u32[]{:S(2)}, u32[]{:S(2)}) %all-to-all-start.1) | async-done | bytes 442400 | tf_op jit(solution)/shard_map/all_to_all | solution.py:52
  71.8 12.7 %all_gather.9 = bf16[1024,64]{0,1:T(8,128)(2,1)} all-gather(bf16[1024,16]{0,1:T(8,128)(2,1)S(1)} %copy-done.11), channel_id=1, replica_groups=mesh['ay'=4,'az'=16,'mx'=4,'mc'=2] {'ay'}, dimensions={1}, use_global_device_ids=true | all-gather | bytes 163840 | tf_op jit(solution)/shard_map/all_gather | solution.py:40
  84.5 20.3 %all-reduce.5.cloned.1.call-done = (f32[3,128,64]{1,2,0:T(8,128)}, f32[3,128,64]{1,2,0:T(8,128)}) async-done(((f32[3,128,64]{1,2,0:T(8,128)}, f32[3,128,64]{1,2,0:T(8,128)}), (f32[3,128,64]{1,2,0:T(8,128)}, f32[3,128,64]{1,2,0:T(8,128)})) %all-reduce.5.cloned.1.call-update) | async-done | bytes 196624 | tf_op jit(solution)/shard_map/psum | solution.py:33
  104.8 17.2 %all-reduce.6 = (bf16[3,128,64]{1,2,0:T(8,128)(2,1)S(1)}, bf16[3,128,64]{1,2,0:T(8,128)(2,1)S(1)}) all-reduce(f32[3,128,64]{1,2,0:T(8,128)} %get-tuple-element.62, f32[3,128,64]{1,2,0:T(8,128)} %get-tuple-element.63), channel_id=1, replica_groups=mesh['ay'=4,'az'=16,'mx'=4,'mc'=2] {'mx'}, use_global_device_ids=true, to_apply=%region_3.4 | all-reduce | flops 49152 | bytes 294912 | tf_op jit(solution)/shard_map/psum | solution.py:33
  123.1 1.6 copy.109
  124.7 1.3 concatenate.19
  127.4 1.3 copy.110
  128.7 12.1 %all-to-all-start.2 = ((f32[3,4,16,1,1152]{4,1,0,3,2:T(4,128)}), f32[3,4,16,1,1152]{4,1,0,3,2:T(4,128)S(1)}, u32[]{:S(2)}, u32[]{:S(2)}) async-start(f32[3,4,16,1,1152]{4,1,0,3,2:T(4,128)} %copy.110), calls=%async_computation.3 | async-start | bytes 1769472 | tf_op jit(solution)/shard_map/all_to_all | solution.py:51
  140.9 15.0 %all_gather.11 = bf16[384,1024]{1,0:T(8,128)(2,1)} all-gather(bf16[384,128]{1,0:T(8,128)(2,1)S(1)} %broadcast_multiply_fusion), channel_id=1, replica_groups=mesh['ay'=4,'az'=16,'mx'=4,'mc'=2] {'mx','mc'}, dimensions={1}, use_global_device_ids=true | all-gather | bytes 884736 | tf_op jit(solution)/shard_map/all_gather | solution.py:103
  156.0 8.7 %all-gather.2.cloned.1.call-done = bf16[1024,1024]{0,1:T(8,128)(2,1)} async-done(((bf16[1024,64]{0,1:T(8,128)(2,1)}), bf16[1024,1024]{0,1:T(8,128)(2,1)}) %all-gather.2.cloned.1.call-update) | async-done | bytes 2097168 | tf_op jit(solution)/shard_map/all_gather | solution.py:41
  164.6 1.8 copy.101
  166.4 1.3 copy-done.2
  167.7 2.4 %convolution_bitcast_fusion = f32[384,1024]{0,1:T(8,128)} fusion(bf16[1024,1024]{0,1:T(8,128)(2,1)S(1)} %bitcast.75, bf16[384,1024]{1,0:T(8,128)(2,1)S(1)} %copy-done), kind=kOutput, calls=%fused_computation.4 | convolution fusion | flops 805306368 | bytes 4456448 | tf_op jit(solution)/shard_map/dot_general | solution.py:121
  170.2 13.4 %all-to-all-done.2 = f32[3,4,16,1,1152]{4,1,0,3,2:T(4,128)S(1)} async-done(((f32[3,4,16,1,1152]{4,1,0,3,2:T(4,128)}), f32[3,4,16,1,1152]{4,1,0,3,2:T(4,128)S(1)}, u32[]{:S(2)}, u32[]{:S(2)}) %all-to-all-start.2) | async-done | bytes 884768 | tf_op jit(solution)/shard_map/all_to_all | solution.py:51
  184.6 4.1 %all-to-all-start.3 = ((f32[3,4,16,1,1152]{4,2,0,3,1:T(8,128)}), f32[3,4,16,1,1152]{4,2,0,3,1:T(8,128)S(1)}, u32[]{:S(2)}, u32[]{:S(2)}) async-start(f32[3,4,16,1,1152]{4,2,0,3,1:T(8,128)} %copy.111), calls=%async_computation.4 | async-start | bytes 1769472 | tf_op jit(solution)/shard_map/all_to_all | solution.py:52
  192.2 1.9 fusion
  194.1 4.6 %all-to-all-done.3 = f32[3,4,16,1,1152]{4,2,0,3,1:T(8,128)S(1)} async-done(((f32[3,4,16,1,1152]{4,2,0,3,1:T(8,128)}), f32[3,4,16,1,1152]{4,2,0,3,1:T(8,128)S(1)}, u32[]{:S(2)}, u32[]{:S(2)}) %all-to-all-start.3) | async-done | bytes 884768 | tf_op jit(solution)/shard_map/all_to_all | solution.py:52
  201.9 1.4 divide_subtract_fusion
  203.3 1.4 reduce-scatter.2.cloned.1.call-done
  (66 shorter events, 19.3 us)
Async XLA Ops:
  8.0 62.6 %copy-start = (bf16[384,1024]{1,0:T(8,128)(2,1)S(1)}, bf16[384,1024]{1,0:T(8,128)(2,1)}, u32[]{:S(2)}) copy-start(bf16[384,1024]{1,0:T(8,128)(2,1)} %param.12) | copy-start | bytes 2359300
  13.2 16.8 %copy-start.14 = (s32[192]{0:T(256)S(1)}, s32[192]{0:T(256)}, u32[]{:S(2)}) copy-start(s32[192]{0:T(256)} %param.22) | copy-start | bytes 2308
  14.7 46.7 %copy-start.10 = (bf16[384,128]{1,0:T(8,128)(2,1)S(1)}, bf16[384,128]{1,0:T(8,128)(2,1)}, u32[]{:S(2)}) copy-start(bf16[384,128]{1,0:T(8,128)(2,1)} %param.13) | copy-start | bytes 294916
  14.7 41.3 %all-to-all-start = ((bf16[4,16,3,1152]{3,0,2,1:T(4,128)(2,1)}), bf16[4,16,3,1152]{3,0,2,1:T(4,128)(2,1)S(1)}, u32[]{:S(2)}, u32[]{:S(2)}) async-start(bf16[4,16,3,1152]{3,0,2,1:T(4,128)(2,1)} %copy.103), calls=%async_computation.1 | async-start | bytes 884736 | tf_op jit(solution)/shard_map/all_to_all | solution.py:51
  56.8 12.3 %all-to-all-start.1 = ((bf16[4,16,3,1152]{3,1,2,0:T(8,128)(2,1)}), bf16[4,16,3,1152]{3,1,2,0:T(8,128)(2,1)S(1)}, u32[]{:S(2)}, u32[]{:S(2)}) async-start(bf16[4,16,3,1152]{3,1,2,0:T(8,128)(2,1)} %copy.104), calls=%async_computation.2 | async-start | bytes 884736 | tf_op jit(solution)/shard_map/all_to_all | solution.py:52
  61.3 43.5 %all-reduce.5.cloned.1.call-start = ((), (), s32[]{:S(2)}) async-start(), calls=%async_computation.7 | async-start | bytes 393216 | tf_op jit(solution)/shard_map/psum | solution.py:33
  69.2 2.5 %copy-start.4 = (bf16[4,16,3,1152]{3,1,0,2:T(8,128)(2,1)}, bf16[4,16,3,1152]{3,1,0,2:T(8,128)(2,1)S(1)}, u32[]{:S(2)}) copy-start(bf16[4,16,3,1152]{3,1,0,2:T(8,128)(2,1)S(1)} %copy.105) | copy-start | bytes 1327108
  69.2 2.5 %copy-start.11 = (bf16[1024,16]{0,1:T(8,128)(2,1)S(1)}, bf16[1024,16]{0,1:T(8,128)(2,1)}, u32[]{:S(2)}) copy-start(bf16[1024,16]{0,1:T(8,128)(2,1)} %param.14) | copy-start | bytes 98308
  71.7 92.9 %all-gather.2.cloned.1.call-start = ((), (), s32[]{:S(2)}) async-start(), calls=%async_computation.5 | async-start | bytes 2228224 | tf_op jit(solution)/shard_map/all_gather | solution.py:41
  128.7 54.9 %all-to-all-start.2 = ((f32[3,4,16,1,1152]{4,1,0,3,2:T(4,128)}), f32[3,4,16,1,1152]{4,1,0,3,2:T(4,128)S(1)}, u32[]{:S(2)}, u32[]{:S(2)}) async-start(f32[3,4,16,1,1152]{4,1,0,3,2:T(4,128)} %copy.110), calls=%async_computation.3 | async-start | bytes 1769472 | tf_op jit(solution)/shard_map/all_to_all | solution.py:51
  140.9 63.9 %reduce-scatter.2.cloned.1.call-start = ((), (), s32[]{:S(2)}) async-start(), calls=%async_computation.6 | async-start | bytes 1769472 | tf_op jit(solution)/shard_map/reduce_scatter | solution.py:126
  166.4 1.3 copy-start.2
  184.6 14.1 %all-to-all-start.3 = ((f32[3,4,16,1,1152]{4,2,0,3,1:T(8,128)}), f32[3,4,16,1,1152]{4,2,0,3,1:T(8,128)S(1)}, u32[]{:S(2)}, u32[]{:S(2)}) async-start(f32[3,4,16,1,1152]{4,2,0,3,1:T(8,128)} %copy.111), calls=%async_computation.4 | async-start | bytes 1769472 | tf_op jit(solution)/shard_map/all_to_all | solution.py:52
  188.7 2.3 %copy-start.6 = (bf16[384,1024]{1,0:T(8,128)(2,1)S(1)}, bf16[384,1024]{1,0:T(8,128)(2,1)}, u32[]{:S(2)}) copy-start(bf16[384,1024]{1,0:T(8,128)(2,1)} %all_gather.11) | copy-start | bytes 2359300
  190.6 1.6 copy-start.3
  198.8 1.1 copy-start.1
  198.8 1.1 copy-start.12
  198.8 1.1 copy-start.13
  199.4 2.5 %copy-start.5 = (bf16[128,1,16,64]{0,3,2,1:T(8,128)(2,1)S(1)}, bf16[128,1,16,64]{0,3,2,1:T(8,128)(2,1)}, u32[]{:S(2)}) copy-start(bf16[128,1,16,64]{0,3,2,1:T(8,128)(2,1)} %param.15) | copy-start | bytes 786436
  199.9 2.0 copy-start.8
  199.9 2.0 copy-start.9
  201.9 2.8 %copy-start.7 = (f32[384,128]{0,1:T(8,128)S(1)}, f32[384,128]{0,1:T(8,128)}, u32[]{:S(2)}) copy-start(f32[384,128]{0,1:T(8,128)} %copy.107) | copy-start | bytes 589828
Sparse Core Ops, SparseCore 0:
  71.8 32.9 all-reduce.4
Sparse Core Ops, SparseCore 1:
  84.6 80.0 all-gather.1
  170.3 34.4 reduce-scatter.1

commit v8 on v6

--- a/solution.py
+++ b/solution.py
@@ -38,13 +38,16 @@
     return whole.reshape(rows, n_y * n_z * cols)
 
 
-def exchange(x, axis):
+def exchange(x, axis, y_first=False):
     n_y = lax.axis_size("ay")
     n_z = lax.axis_size("az")
     shape = x.shape
     x = x.reshape(shape[:axis] + (n_y, n_z, shape[axis] // (n_y * n_z)) + shape[axis + 1 :])
+    if y_first:
+        x = lax.all_to_all(x, "ay", split_axis=axis, concat_axis=axis, tiled=True)
     x = lax.all_to_all(x, "az", split_axis=axis + 1, concat_axis=axis + 1, tiled=True)
-    x = lax.all_to_all(x, "ay", split_axis=axis, concat_axis=axis, tiled=True)
+    if not y_first:
+        x = lax.all_to_all(x, "ay", split_axis=axis, concat_axis=axis, tiled=True)
     return x.reshape(shape)
 
 
@@ -146,7 +149,7 @@
     grads = jnp.concatenate(
         [home_down.reshape(tiles_here, n_adapter, row_part * rank), local_up_weight], axis=2
     )
-    grads = exchange(grads, 1).transpose(1, 0, 2).reshape(tile_total, -1)
+    grads = exchange(grads, 1, y_first=True).transpose(1, 0, 2).reshape(tile_total, -1)
     arrived_down = grads[:, : row_part * rank]
     arrived_up = grads[:, row_part * rank :]
     selector = (adapter_ids[:, None] == tile_adapter_slot[None, :]).astype(jnp.float32)

time: 182 us -> 193 us (1.060); the launches traced: 181 us -> 189 us
  blocking collectives: 51.4 us -> 66.9 us
  waiting for transfers between devices: 50.6 us -> 47.4 us
  starting transfers between devices: 30.7 us -> 27.6 us
    all_to_all x0 -> x1, blocking collectives: none -> 16.9 us  [exchange(): x = lax.all_to_all(x, 'ay', split_axis=axis, concat_axis=axis, tiled=True)]
    reduce_scatter x1, waiting for transfers between devices: 0.01 us -> 9.9 us  [shards(): lax.psum_scatter(frozen_part, 'mp', scatter_dimension=1, tiled=True)]
    all_gather x1, waiting for transfers between devices: 6.22 us -> 0.01 us  [gather_weight(): whole = lax.all_gather(first, 'az', axis=1, tiled=True)]
    all_to_all x2 -> x1, waiting for transfers between devices: 12.6 us -> 7.45 us  [exchange(): x = lax.all_to_all(x, 'ay', split_axis=axis, concat_axis=axis, tiled=True)]
    all_to_all x2 -> x1, starting transfers between devices: 8.26 us -> 4.46 us  [exchange(): x = lax.all_to_all(x, 'ay', split_axis=axis, concat_axis=axis, tiled=True)]
  transfers between devices with their start and end apart: 6 -> 5, of which waited for: 5 -> 4; matrix products, arithmetic and copies ran while one was open for 13% -> 12% of each run, Pallas kernels for 0% -> 0%
where the time goes in v8:
time: 193 us; the launch traced here: 189 us
  blocking collectives  66.9 us (35%)
  waiting for transfers between devices  47.4 us (25%)
  starting transfers between devices  27.6 us (14%)
  local copies, waits for them, and re-layouts  18.1 us (9%)
  between operations  14.4 us (7%)
  matrix products  9.64 us (5%)
  other arithmetic  4.97 us (3%)
    all_to_all x2, waiting for transfers between devices, exchange(): lax.all_to_all(x, 'az', split_axis=axis + 1, concat_axis=axis + 1, tiled=...  30 us
    psum x1, blocking collectives, shards(): down_sum = lax.psum(down_part, 'mp')  23.1 us
    all_to_all x2, starting transfers between devices, exchange(): lax.all_to_all(x, 'az', split_axis=axis + 1, concat_axis=axis + 1, tiled=...  23 us
    all_to_all x1, blocking collectives, exchange(): x = lax.all_to_all(x, 'ay', split_axis=axis, concat_axis=axis, tiled=True)  16.9 us
    all_gather x1, blocking collectives, shards(): masked_full = lax.all_gather(masked_own, 'mp', axis=1, tiled=True)  13.6 us
    all_gather x1, blocking collectives, gather_weight(): first = lax.all_gather(value_weight, 'ay', axis=1, tiled=True)  13.3 us
    reduce_scatter x1, waiting for transfers between devices, shards(): lax.psum_scatter(frozen_part, 'mp', scatter_dimension=1, tiled=True)  9.9 us
    all_to_all x1, waiting for transfers between devices, exchange(): x = lax.all_to_all(x, 'ay', split_axis=axis, concat_axis=axis, tiled=True)  7.45 us
  transfers between devices with their start and end apart: 5, of which 4 were waited for; matrix products, arithmetic and copies ran while one was open for 12% of the time, Pallas kernels for 0%

profile of v8, /device:TPU:6, one launch (start us, length us, event | category | flops | bytes accessed | tf_op | source)
XLA Modules:
  0.0 189.0 jit_solution(11753330698785855317)
XLA Ops:
  8.2 1.5 gather_fusion.1
  9.7 1.4 copy.102
  12.7 1.2 copy.103
  13.8 15.3 %all-to-all-start = ((bf16[4,16,3,1152]{3,0,2,1:T(4,128)(2,1)}), bf16[4,16,3,1152]{3,0,2,1:T(4,128)(2,1)S(1)}, u32[]{:S(2)}, u32[]{:S(2)}) async-start(bf16[4,16,3,1152]{3,0,2,1:T(4,128)(2,1)} %copy.103), calls=%async_computation.1 | async-start | bytes 884736 | tf_op jit(solution)/shard_map/all_to_all | solution.py:48
  29.2 13.3 %all_gather.9 = bf16[1024,64]{0,1:T(8,128)(2,1)} all-gather(bf16[1024,16]{0,1:T(8,128)(2,1)S(1)} %copy-done.11), channel_id=1, replica_groups=mesh['ay'=4,'az'=16,'mp'=8] {'ay'}, dimensions={1}, use_global_device_ids=true | all-gather | bytes 163840 | tf_op jit(solution)/shard_map/all_gather | solution.py:35
  42.6 12.6 %all-to-all-done = bf16[4,16,3,1152]{3,0,2,1:T(4,128)(2,1)S(1)} async-done(((bf16[4,16,3,1152]{3,0,2,1:T(4,128)(2,1)}), bf16[4,16,3,1152]{3,0,2,1:T(4,128)(2,1)S(1)}, u32[]{:S(2)}, u32[]{:S(2)}) %all-to-all-start) | async-done | bytes 442400 | tf_op jit(solution)/shard_map/all_to_all | solution.py:48
  56.0 4.5 %all-to-all-start.1 = ((bf16[4,16,3,1152]{3,1,2,0:T(8,128)(2,1)}), bf16[4,16,3,1152]{3,1,2,0:T(8,128)(2,1)S(1)}, u32[]{:S(2)}, u32[]{:S(2)}) async-start(bf16[4,16,3,1152]{3,1,2,0:T(8,128)(2,1)} %copy.104), calls=%async_computation.2 | async-start | bytes 884736 | tf_op jit(solution)/shard_map/all_to_all | solution.py:50
  60.7 7.4 %all-to-all-done.1 = bf16[4,16,3,1152]{3,1,2,0:T(8,128)(2,1)S(1)} async-done(((bf16[4,16,3,1152]{3,1,2,0:T(8,128)(2,1)}), bf16[4,16,3,1152]{3,1,2,0:T(8,128)(2,1)S(1)}, u32[]{:S(2)}, u32[]{:S(2)}) %all-to-all-start.1) | async-done | bytes 442400 | tf_op jit(solution)/shard_map/all_to_all | solution.py:50
  69.3 23.1 %all-reduce.2 = (bf16[3,128,64]{1,2,0:T(8,128)(2,1)S(1)}, bf16[3,128,64]{1,2,0:T(8,128)(2,1)S(1)}) all-reduce(f32[3,128,64]{1,2,0:T(8,128)S(1)} %convolution_bitcast_fusion.2, f32[3,128,64]{1,2,0:T(8,128)S(1)} %convolution_multiply_fusion.2), channel_id=1, replica_groups=mesh['ay'=4,'az'=16,'mp'=8] {'mp'}, use_global_device_ids=true, to_apply=%region_2.3 | all-reduce | flops 49152 | bytes 294912 | tf_op jit(solution)/shard_map/psum | solution.py:120
  93.6 1.6 copy.109
  95.2 1.3 concatenate.19
  96.6 1.2 pad_maximum_fusion
  97.9 16.9 %all_to_all.20 = f32[3,4,16,1,1152]{4,2,0,3,1:T(8,128)S(1)} all-to-all(f32[3,4,16,1,1152]{4,2,0,3,1:T(8,128)S(1)} %copy.110), channel_id=1, replica_groups=mesh['ay'=4,'az'=16,'mp'=8] {'ay'}, dimensions={1} | all-to-all | bytes 1769472 | tf_op jit(solution)/shard_map/all_to_all | solution.py:47
  114.9 1.3 copy.111
  116.1 7.7 %all-to-all-start.3 = ((f32[3,4,16,1,1152]{4,1,0,3,2:T(4,128)}), f32[3,4,16,1,1152]{4,1,0,3,2:T(4,128)S(1)}, u32[]{:S(2)}, u32[]{:S(2)}) async-start(f32[3,4,16,1,1152]{4,1,0,3,2:T(4,128)} %copy.111), calls=%async_computation.4 | async-start | bytes 1769472 | tf_op jit(solution)/shard_map/all_to_all | solution.py:48
  123.9 13.6 %all_gather.11 = bf16[384,1024]{1,0:T(8,128)(2,1)} all-gather(bf16[384,128]{1,0:T(8,128)(2,1)S(1)} %broadcast_multiply_fusion), channel_id=1, replica_groups=mesh['ay'=4,'az'=16,'mp'=8] {'mp'}, dimensions={1}, use_global_device_ids=true | all-gather | bytes 884736 | tf_op jit(solution)/shard_map/all_gather | solution.py:93
  137.5 1.8 copy.101
  139.3 1.3 copy-done.2
  140.6 2.4 %convolution_bitcast_fusion = f32[384,1024]{0,1:T(8,128)} fusion(bf16[1024,1024]{0,1:T(8,128)(2,1)S(1)} %bitcast.75, bf16[384,1024]{1,0:T(8,128)(2,1)S(1)} %copy-done), kind=kOutput, calls=%fused_computation.4 | convolution fusion | flops 805306368 | bytes 4456448 | tf_op jit(solution)/shard_map/dot_general | solution.py:111
  145.4 1.2 copy-done.3
  146.6 1.9 fusion
  148.5 17.5 %all-to-all-done.3 = f32[3,4,16,1,1152]{4,1,0,3,2:T(4,128)S(1)} async-done(((f32[3,4,16,1,1152]{4,1,0,3,2:T(4,128)}), f32[3,4,16,1,1152]{4,1,0,3,2:T(4,128)S(1)}, u32[]{:S(2)}, u32[]{:S(2)}) %all-to-all-start.3) | async-done | bytes 884768 | tf_op jit(solution)/shard_map/all_to_all | solution.py:48
  169.2 1.4 divide_subtract_fusion
  170.5 9.9 %reduce-scatter.2.cloned.1.call-done = f32[384,128]{0,1:T(8,128)} async-done(((f32[384,1024]{0,1:T(8,128)}), f32[384,128]{0,1:T(8,128)}) %reduce-scatter.2.cloned.1.call-update) | async-done | bytes 196624 | tf_op jit(solution)/shard_map/reduce_scatter | solution.py:116
  (62 shorter events, 13.5 us)
Async XLA Ops:
  7.2 61.5 %copy-start = (bf16[384,1024]{1,0:T(8,128)(2,1)S(1)}, bf16[384,1024]{1,0:T(8,128)(2,1)}, u32[]{:S(2)}) copy-start(bf16[384,1024]{1,0:T(8,128)(2,1)} %param.12) | copy-start | bytes 2359300
  12.4 16.9 %copy-start.11 = (bf16[1024,16]{0,1:T(8,128)(2,1)S(1)}, bf16[1024,16]{0,1:T(8,128)(2,1)}, u32[]{:S(2)}) copy-start(bf16[1024,16]{0,1:T(8,128)(2,1)} %param.14) | copy-start | bytes 98308
  12.4 30.2 %copy-start.14 = (s32[192]{0:T(256)S(1)}, s32[192]{0:T(256)}, u32[]{:S(2)}) copy-start(s32[192]{0:T(256)} %param.22) | copy-start | bytes 2308
  13.8 46.7 %copy-start.10 = (bf16[384,128]{1,0:T(8,128)(2,1)S(1)}, bf16[384,128]{1,0:T(8,128)(2,1)}, u32[]{:S(2)}) copy-start(bf16[384,128]{1,0:T(8,128)(2,1)} %param.13) | copy-start | bytes 294916
  13.8 41.3 %all-to-all-start = ((bf16[4,16,3,1152]{3,0,2,1:T(4,128)(2,1)}), bf16[4,16,3,1152]{3,0,2,1:T(4,128)(2,1)S(1)}, u32[]{:S(2)}, u32[]{:S(2)}) async-start(bf16[4,16,3,1152]{3,0,2,1:T(4,128)(2,1)} %copy.103), calls=%async_computation.1 | async-start | bytes 884736 | tf_op jit(solution)/shard_map/all_to_all | solution.py:48
  29.2 108.3 %all-gather.2.cloned.1.call-start = ((), (), s32[]{:S(2)}) async-start(), calls=%async_computation.5 | async-start | bytes 2228224 | tf_op jit(solution)/shard_map/all_gather | solution.py:36
  56.0 12.1 %all-to-all-start.1 = ((bf16[4,16,3,1152]{3,1,2,0:T(8,128)(2,1)}), bf16[4,16,3,1152]{3,1,2,0:T(8,128)(2,1)S(1)}, u32[]{:S(2)}, u32[]{:S(2)}) async-start(bf16[4,16,3,1152]{3,1,2,0:T(8,128)(2,1)} %copy.104), calls=%async_computation.2 | async-start | bytes 884736 | tf_op jit(solution)/shard_map/all_to_all | solution.py:50
  68.2 1.0 copy-start.4
  116.1 49.8 %all-to-all-start.3 = ((f32[3,4,16,1,1152]{4,1,0,3,2:T(4,128)}), f32[3,4,16,1,1152]{4,1,0,3,2:T(4,128)S(1)}, u32[]{:S(2)}, u32[]{:S(2)}) async-start(f32[3,4,16,1,1152]{4,1,0,3,2:T(4,128)} %copy.111), calls=%async_computation.4 | async-start | bytes 1769472 | tf_op jit(solution)/shard_map/all_to_all | solution.py:48
  123.8 56.6 %reduce-scatter.2.cloned.1.call-start = ((), (), s32[]{:S(2)}) async-start(), calls=%async_computation.6 | async-start | bytes 1769472 | tf_op jit(solution)/shard_map/reduce_scatter | solution.py:116
  139.3 1.3 copy-start.2
  143.0 2.4 %copy-start.6 = (bf16[384,1024]{1,0:T(8,128)(2,1)S(1)}, bf16[384,1024]{1,0:T(8,128)(2,1)}, u32[]{:S(2)}) copy-start(bf16[384,1024]{1,0:T(8,128)(2,1)} %all_gather.11) | copy-start | bytes 2359300
  145.0 1.6 copy-start.3
  166.0 1.1 copy-start.1
  166.0 1.1 copy-start.12
  166.0 1.1 copy-start.13
  166.7 2.5 %copy-start.5 = (bf16[128,1,16,64]{0,3,2,1:T(8,128)(2,1)S(1)}, bf16[128,1,16,64]{0,3,2,1:T(8,128)(2,1)}, u32[]{:S(2)}) copy-start(bf16[128,1,16,64]{0,3,2,1:T(8,128)(2,1)} %param.15) | copy-start | bytes 786436
  167.1 2.0 %copy-start.8 = (f32[128,1,16,64]{0,3,2,1:T(8,128)S(1)}, f32[128,1,16,64]{0,3,2,1:T(8,128)}, u32[]{:S(2)}) copy-start(f32[128,1,16,64]{0,3,2,1:T(8,128)} %param.16) | copy-start | bytes 1572868
  167.1 2.0 %copy-start.9 = (f32[128,1,16,64]{0,3,2,1:T(8,128)S(1)}, f32[128,1,16,64]{0,3,2,1:T(8,128)}, u32[]{:S(2)}) copy-start(f32[128,1,16,64]{0,3,2,1:T(8,128)} %param.17) | copy-start | bytes 1572868
  169.1 11.3 %copy-start.7 = (f32[384,128]{0,1:T(8,128)S(1)}, f32[384,128]{0,1:T(8,128)}, u32[]{:S(2)}) copy-start(f32[384,128]{0,1:T(8,128)} %copy.107) | copy-start | bytes 589828
Sparse Core Ops, SparseCore 0:
  42.6 73.1 all-gather.1
  143.2 37.2 reduce-scatter.1

commit v9 on v6

--- a/solution.py
+++ b/solution.py
@@ -28,11 +28,10 @@
 ADAPTER = ("ay", "az")
 
 
-def gather_weight(value_weight):
-    rows, cols = value_weight.shape
+def gather_weight(first, cols):
+    rows = first.shape[0]
     n_y = lax.axis_size("ay")
     n_z = lax.axis_size("az")
-    first = lax.all_gather(value_weight, "ay", axis=1, tiled=True)
     whole = lax.all_gather(first, "az", axis=1, tiled=True)
     whole = whole.reshape(rows, n_z, n_y, cols).transpose(0, 2, 1, 3)
     return whole.reshape(rows, n_y * n_z * cols)
@@ -94,6 +93,8 @@
     sent_down = down_store[:, 0][tile_adapter_slot].reshape(tile_total, row_part * rank)
     sent_up = up_store[tile_adapter_slot].reshape(tile_total, head_cols)
     sent = jnp.concatenate([sent_down, sent_up], axis=1)
+    w_first = lax.all_gather(value_weight, "ay", axis=1, tiled=True)
+    w_first, sent = lax.optimization_barrier((w_first, sent))
     arrived = exchange(sent, 0)
     arrived = arrived.reshape(n_adapter, tiles_here, row_part * rank + head_cols)
     down_panel = (
@@ -103,7 +104,7 @@
         .reshape(tiles_here, n_adapter * row_part, rank)
     )
     up_panel = arrived[:, :, row_part * rank :].transpose(1, 0, 2)
-    w_full, masked_full = lax.optimization_barrier((gather_weight(value_weight), masked_full))
+    w_full, masked_full = lax.optimization_barrier((gather_weight(w_first, value_weight.shape[1]), masked_full))
     token_tiles = tokens.reshape(tiles_here, TILE, feat_part)
     frozen_part = jnp.dot(
         tokens,

time: 182 us -> 191 us (1.049)
  waiting for transfers between devices: 50.6 us -> 59 us
    all_to_all x2, waiting for transfers between devices: 31.7 us -> 46.3 us  [exchange(): lax.all_to_all(x, 'az', split_axis=axis + 1, concat_axis=axis + 1, tiled=...]
    all_gather x1, waiting for transfers between devices: 6.22 us -> 0.01 us  [gather_weight(): whole = lax.all_gather(first, 'az', axis=1, tiled=True)]
    unnamed x32 -> x30, local copies, waits for them, and re-layouts: 4.74 us -> 4.73 us
  transfers between devices with their start and end apart: 6 -> 6, of which waited for: 5 -> 4; matrix products, arithmetic and copies ran while one was open for 13% -> 12% of each run, Pallas kernels for 0% -> 0%
where the time goes in v9:
time: 191 us; the launch traced here: 190 us
  waiting for transfers between devices  59 us (31%)
  blocking collectives  53 us (28%)
  starting transfers between devices  29.4 us (15%)
  local copies, waits for them, and re-layouts  19.6 us (10%)
  between operations  14.4 us (8%)
  matrix products  9.63 us (5%)
  other arithmetic  4.72 us (2%)
    all_to_all x2, waiting for transfers between devices, exchange(): lax.all_to_all(x, 'az', split_axis=axis + 1, concat_axis=axis + 1, tiled=...  46.3 us
    psum x1, blocking collectives, shards(): down_sum = lax.psum(down_part, 'mp')  23.7 us
    all_to_all x2, starting transfers between devices, exchange(): lax.all_to_all(x, 'az', split_axis=axis + 1, concat_axis=axis + 1, tiled=...  22.2 us
    all_gather x1, blocking collectives, shards(): masked_full = lax.all_gather(masked_own, 'mp', axis=1, tiled=True)  15.1 us
    all_gather x1, blocking collectives, shards(): w_first = lax.all_gather(value_weight, 'ay', axis=1, tiled=True)  14.2 us
    all_to_all x2, waiting for transfers between devices, exchange(): x = lax.all_to_all(x, 'ay', split_axis=axis, concat_axis=axis, tiled=True)  12 us
    all_to_all x2, starting transfers between devices, exchange(): x = lax.all_to_all(x, 'ay', split_axis=axis, concat_axis=axis, tiled=True)  7.15 us
    unnamed x30, local copies, waits for them, and re-layouts  4.73 us
  transfers between devices with their start and end apart: 6, of which 4 were waited for; matrix products, arithmetic and copies ran while one was open for 12% of the time, Pallas kernels for 0%

profile of v9, /device:TPU:6, one launch (start us, length us, event | category | flops | bytes accessed | tf_op | source)
XLA Modules:
  0.0 189.8 jit_solution(6669583274257211116)
XLA Ops:
  7.2 14.2 %all_gather.9 = bf16[1024,64]{0,1:T(8,128)(2,1)} all-gather(bf16[1024,16]{0,1:T(8,128)(2,1)} %param.14), channel_id=1, replica_groups=mesh['ay'=4,'az'=16,'mp'=8] {'ay'}, dimensions={1}, use_global_device_ids=true | all-gather | bytes 163840 | tf_op jit(solution)/shard_map/all_gather | solution.py:96
  22.3 1.5 gather_fusion.1
  23.9 1.4 copy.109
  27.3 1.2 copy.114
  28.5 15.3 %all-to-all-start = ((bf16[4,16,3,1152]{3,0,2,1:T(4,128)(2,1)}), bf16[4,16,3,1152]{3,0,2,1:T(4,128)(2,1)S(1)}, u32[]{:S(2)}, u32[]{:S(2)}) async-start(bf16[4,16,3,1152]{3,0,2,1:T(4,128)(2,1)} %copy.114), calls=%async_computation.1 | async-start | bytes 884736 | tf_op jit(solution)/shard_map/all_to_all | solution.py:45
  44.7 21.5 %all-to-all-done = bf16[4,16,3,1152]{3,0,2,1:T(4,128)(2,1)S(1)} async-done(((bf16[4,16,3,1152]{3,0,2,1:T(4,128)(2,1)}), bf16[4,16,3,1152]{3,0,2,1:T(4,128)(2,1)S(1)}, u32[]{:S(2)}, u32[]{:S(2)}) %all-to-all-start) | async-done | bytes 442400 | tf_op jit(solution)/shard_map/all_to_all | solution.py:45
  67.0 3.5 %all-to-all-start.1 = ((bf16[4,16,3,1152]{3,1,2,0:T(8,128)(2,1)}), bf16[4,16,3,1152]{3,1,2,0:T(8,128)(2,1)S(1)}, u32[]{:S(2)}, u32[]{:S(2)}) async-start(bf16[4,16,3,1152]{3,1,2,0:T(8,128)(2,1)} %copy.115), calls=%async_computation.2 | async-start | bytes 884736 | tf_op jit(solution)/shard_map/all_to_all | solution.py:46
  70.7 7.4 %all-to-all-done.1 = bf16[4,16,3,1152]{3,1,2,0:T(8,128)(2,1)S(1)} async-done(((bf16[4,16,3,1152]{3,1,2,0:T(8,128)(2,1)}), bf16[4,16,3,1152]{3,1,2,0:T(8,128)(2,1)S(1)}, u32[]{:S(2)}, u32[]{:S(2)}) %all-to-all-start.1) | async-done | bytes 442400 | tf_op jit(solution)/shard_map/all_to_all | solution.py:46
  79.3 23.7 %all-reduce.2 = (bf16[3,128,64]{1,2,0:T(8,128)(2,1)S(1)}, bf16[3,128,64]{1,2,0:T(8,128)(2,1)S(1)}) all-reduce(f32[3,128,64]{1,2,0:T(8,128)S(1)} %convolution_bitcast_fusion.2, f32[3,128,64]{1,2,0:T(8,128)S(1)} %convolution_multiply_fusion.2), channel_id=1, replica_groups=mesh['ay'=4,'az'=16,'mp'=8] {'mp'}, use_global_device_ids=true, to_apply=%region_2.3 | all-reduce | flops 49152 | bytes 294912 | tf_op jit(solution)/shard_map/psum | solution.py:118
  104.1 1.6 copy.120
  105.7 1.3 concatenate.12
  107.2 1.2 pad_maximum_fusion
  108.4 1.3 copy.121
  109.7 6.8 %all-to-all-start.2 = ((f32[3,4,16,1,1152]{4,1,0,3,2:T(4,128)}), f32[3,4,16,1,1152]{4,1,0,3,2:T(4,128)S(1)}, u32[]{:S(2)}, u32[]{:S(2)}) async-start(f32[3,4,16,1,1152]{4,1,0,3,2:T(4,128)} %copy.121), calls=%async_computation.3 | async-start | bytes 1769472 | tf_op jit(solution)/shard_map/all_to_all | solution.py:45
  116.6 15.1 %all_gather.11 = bf16[384,1024]{1,0:T(8,128)(2,1)} all-gather(bf16[384,128]{1,0:T(8,128)(2,1)S(1)} %broadcast_multiply_fusion), channel_id=1, replica_groups=mesh['ay'=4,'az'=16,'mp'=8] {'mp'}, dimensions={1}, use_global_device_ids=true | all-gather | bytes 884736 | tf_op jit(solution)/shard_map/all_gather | solution.py:89
  131.7 1.8 copy.112
  133.5 1.3 copy-done.2
  134.8 2.4 %convolution_bitcast_fusion = f32[384,1024]{0,1:T(8,128)} fusion(bf16[1024,1024]{0,1:T(8,128)(2,1)S(1)} %bitcast.76, bf16[384,1024]{1,0:T(8,128)(2,1)S(1)} %copy-done), kind=kOutput, calls=%fused_computation.4 | convolution fusion | flops 805306368 | bytes 4456448 | tf_op jit(solution)/shard_map/dot_general | solution.py:109
  137.2 24.7 %all-to-all-done.2 = f32[3,4,16,1,1152]{4,1,0,3,2:T(4,128)S(1)} async-done(((f32[3,4,16,1,1152]{4,1,0,3,2:T(4,128)}), f32[3,4,16,1,1152]{4,1,0,3,2:T(4,128)S(1)}, u32[]{:S(2)}, u32[]{:S(2)}) %all-to-all-start.2) | async-done | bytes 884768 | tf_op jit(solution)/shard_map/all_to_all | solution.py:45
  162.9 3.7 %all-to-all-start.3 = ((f32[3,4,16,1,1152]{4,2,0,3,1:T(8,128)}), f32[3,4,16,1,1152]{4,2,0,3,1:T(8,128)S(1)}, u32[]{:S(2)}, u32[]{:S(2)}) async-start(f32[3,4,16,1,1152]{4,2,0,3,1:T(8,128)} %copy.122), calls=%async_computation.4 | async-start | bytes 1769472 | tf_op jit(solution)/shard_map/all_to_all | solution.py:46
  169.0 1.2 copy-done.3
  170.2 1.9 fusion
  172.1 4.6 %all-to-all-done.3 = f32[3,4,16,1,1152]{4,2,0,3,1:T(8,128)S(1)} async-done(((f32[3,4,16,1,1152]{4,2,0,3,1:T(8,128)}), f32[3,4,16,1,1152]{4,2,0,3,1:T(8,128)S(1)}, u32[]{:S(2)}, u32[]{:S(2)}) %all-to-all-start.3) | async-done | bytes 884768 | tf_op jit(solution)/shard_map/all_to_all | solution.py:46
  179.9 1.4 divide_subtract_fusion
  (63 shorter events, 15.4 us)
Async XLA Ops:
  7.2 71.5 %copy-start = (bf16[384,1024]{1,0:T(8,128)(2,1)S(1)}, bf16[384,1024]{1,0:T(8,128)(2,1)}, u32[]{:S(2)}) copy-start(bf16[384,1024]{1,0:T(8,128)(2,1)} %param.12) | copy-start | bytes 2359300
  27.1 17.5 %copy-start.13 = (s32[192]{0:T(256)S(1)}, s32[192]{0:T(256)}, u32[]{:S(2)}) copy-start(s32[192]{0:T(256)} %param.22) | copy-start | bytes 2308
  28.5 42.1 %copy-start.10 = (bf16[384,128]{1,0:T(8,128)(2,1)S(1)}, bf16[384,128]{1,0:T(8,128)(2,1)}, u32[]{:S(2)}) copy-start(bf16[384,128]{1,0:T(8,128)(2,1)} %param.13) | copy-start | bytes 294916
  28.5 37.7 %all-to-all-start = ((bf16[4,16,3,1152]{3,0,2,1:T(4,128)(2,1)}), bf16[4,16,3,1152]{3,0,2,1:T(4,128)(2,1)S(1)}, u32[]{:S(2)}, u32[]{:S(2)}) async-start(bf16[4,16,3,1152]{3,0,2,1:T(4,128)(2,1)} %copy.114), calls=%async_computation.1 | async-start | bytes 884736 | tf_op jit(solution)/shard_map/all_to_all | solution.py:45
  43.8 87.9 %all-gather.2.cloned.1.call-start = ((), (), s32[]{:S(2)}) async-start(), calls=%async_computation.5 | async-start | bytes 2228224 | tf_op jit(solution)/shard_map/all_gather | solution.py:35
  67.0 11.1 %all-to-all-start.1 = ((bf16[4,16,3,1152]{3,1,2,0:T(8,128)(2,1)}), bf16[4,16,3,1152]{3,1,2,0:T(8,128)(2,1)S(1)}, u32[]{:S(2)}, u32[]{:S(2)}) async-start(bf16[4,16,3,1152]{3,1,2,0:T(8,128)(2,1)} %copy.115), calls=%async_computation.2 | async-start | bytes 884736 | tf_op jit(solution)/shard_map/all_to_all | solution.py:46
  78.1 1.0 copy-start.4
  109.7 52.3 %all-to-all-start.2 = ((f32[3,4,16,1,1152]{4,1,0,3,2:T(4,128)}), f32[3,4,16,1,1152]{4,1,0,3,2:T(4,128)S(1)}, u32[]{:S(2)}, u32[]{:S(2)}) async-start(f32[3,4,16,1,1152]{4,1,0,3,2:T(4,128)} %copy.121), calls=%async_computation.3 | async-start | bytes 1769472 | tf_op jit(solution)/shard_map/all_to_all | solution.py:45
  116.5 64.7 %reduce-scatter.2.cloned.1.call-start = ((), (), s32[]{:S(2)}) async-start(), calls=%async_computation.6 | async-start | bytes 1769472 | tf_op jit(solution)/shard_map/reduce_scatter | solution.py:114
  133.5 1.3 copy-start.2
  162.9 13.7 %all-to-all-start.3 = ((f32[3,4,16,1,1152]{4,2,0,3,1:T(8,128)}), f32[3,4,16,1,1152]{4,2,0,3,1:T(8,128)S(1)}, u32[]{:S(2)}, u32[]{:S(2)}) async-start(f32[3,4,16,1,1152]{4,2,0,3,1:T(8,128)} %copy.122), calls=%async_computation.4 | async-start | bytes 1769472 | tf_op jit(solution)/shard_map/all_to_all | solution.py:46
  166.6 2.4 %copy-start.6 = (bf16[384,1024]{1,0:T(8,128)(2,1)S(1)}, bf16[384,1024]{1,0:T(8,128)(2,1)}, u32[]{:S(2)}) copy-start(bf16[384,1024]{1,0:T(8,128)(2,1)} %all_gather.11) | copy-start | bytes 2359300
  168.6 1.6 copy-start.3
  176.7 1.1 copy-start.1
  176.7 1.1 copy-start.11
  176.7 1.1 copy-start.12
  177.4 2.5 %copy-start.5 = (bf16[128,1,16,64]{0,3,2,1:T(8,128)(2,1)S(1)}, bf16[128,1,16,64]{0,3,2,1:T(8,128)(2,1)}, u32[]{:S(2)}) copy-start(bf16[128,1,16,64]{0,3,2,1:T(8,128)(2,1)} %param.15) | copy-start | bytes 786436
  177.8 2.0 %copy-start.8 = (f32[128,1,16,64]{0,3,2,1:T(8,128)S(1)}, f32[128,1,16,64]{0,3,2,1:T(8,128)}, u32[]{:S(2)}) copy-start(f32[128,1,16,64]{0,3,2,1:T(8,128)} %param.16) | copy-start | bytes 1572868
  177.9 2.0 %copy-start.9 = (f32[128,1,16,64]{0,3,2,1:T(8,128)S(1)}, f32[128,1,16,64]{0,3,2,1:T(8,128)}, u32[]{:S(2)}) copy-start(f32[128,1,16,64]{0,3,2,1:T(8,128)} %param.17) | copy-start | bytes 1572868
  179.9 1.4 copy-start.7
Sparse Core Ops, SparseCore 0:
  46.7 72.6 all-gather.1
  137.4 38.7 reduce-scatter.1
